TPU v7x, 256 devices: a whole 4x4x8 slice. The times are simulated.
256 devices in a mesh: req: 32 (over z_hi, y, core), tp: 8 (over z_lo, x).
Axes of the slice: x: 4, y: 4, z: 8 (z_hi: 4, z_lo: 2; z = z_hi * 2 + z_lo), core: 2. Of those that a mesh axis runs over, the one named last changes fastest.
Arguments:
- hidden_states: bfloat16 [4096, 2880], P('req', 'tp'), may hold values from -64 to 64
- attn_gain: float32 [2880], replicated, may hold values from 0.1 to 1.9
- query_weight: bfloat16 [2880, 4096], P(None, 'tp'), may hold values from -0.109375 to 0.109375
- key_value_weight: bfloat16 [2880, 1024], P(None, 'tp'), may hold values from -0.3125 to 0.3125
- sink_logits: float32 [64], P('tp'), may hold values from 4 to 11
- prefix_cache: bfloat16 [32768, 1024], P('req', 'tp'), may hold values from -512 to 512
- out_weight: bfloat16 [4096, 2880], P('tp'), may hold values from -0.125 to 0.125
- ffn_gain: float32 [2880], replicated, may hold values from 0.1 to 1.9
- router_weight: bfloat16 [2880, 32], P('tp'), may hold values from -0.21875 to 0.21875
- gate_up_weight: bfloat16 [32, 2880, 2, 2880], P('req', None, None, 'tp'), may hold values from -0.4375 to 0.4375
- down_weight: bfloat16 [32, 2880, 2880], P('req', 'tp'), may hold values from -0.013671875 to 0.013671875
- route_ids: int32 [4096, 4], P('req'), may hold values from 0 to 31, all different within a row; in each aligned block of 128 rows (0 to 127, 128 to 255, ...) at most 24 rows name the same one
- prefix_group: int32 [32], replicated, may hold values from 0 to 1
- suffix_lengths: int32 [32], replicated, may hold values from 1 to 128, 2048 in all
Outputs:
- attn_out: bfloat16 [4096, 2880], P('req', 'tp')
- moe_out: bfloat16 [4096, 2880], P('req', 'tp')
Inputs may be any that keep to these rules, and one draw needn't show every extreme that they name: `route_ids`: among the 128 tokens of one request no expert is named more than 24 times; some expert is named exactly 24 times in some requests. `suffix_lengths`: rows of a request from its length on are padding; the longest request fills all 128 slots.
All inputs are finite; a program needn't handle non-finite values.
Results may differ from a plain program's by a relative error of at most 0.02.
The roundings to bfloat16 on the way count: a program that leaves them out, or rounds other values in their place, can miss the bound.
Values may be sent and summed in bfloat16 or wider, within the bound.
No kernel may reach another device: no remote copies, remote signals or barrier semaphores. Data moves between devices by JAX's collectives and lax.ppermute only.
A program may use at most 128 MiB of HBM per device.

v0:
```python
import jax
import jax.numpy as jnp
from jax import lax
from jax.sharding import PartitionSpec as P

D = 2880
HEAD = 64


rope_base = 150000.0
norm_eps = 1e-05
clamp_limit = 7.0
glu_alpha = 1.702


def rms_rows(values, gain):
    wide = values.astype(jnp.float32)
    factor = lax.rsqrt(jnp.mean(wide * wide, axis=1, keepdims=True) + norm_eps)
    return (wide * factor * gain).astype(jnp.bfloat16)


def rotate(values, positions):
    half_size = values.shape[-1] // 2
    powers = jnp.arange(half_size, dtype=jnp.float32) * (-2.0 / values.shape[-1])
    angles = positions[:, None, None] * rope_base**powers
    cosine = jnp.cos(angles)
    sine_part = jnp.sin(angles)
    first_half = values[..., :half_size]
    second_half = values[..., half_size:]
    return jnp.concatenate(
        [
            first_half * cosine - second_half * sine_part,
            second_half * cosine + first_half * sine_part,
        ],
        axis=-1,
    )


def local(
    hidden_states,
    attn_gain,
    query_weight,
    key_value_weight,
    sink_logits,
    prefix_cache,
    out_weight,
    ffn_gain,
    router_weight,
    gate_up_weight,
    down_weight,
    route_ids,
    prefix_group,
    suffix_lengths,
):
    token_count = hidden_states.shape[0]
    head_size = HEAD
    model_width = D
    local_heads = query_weight.shape[1] // head_size
    local_kv = key_value_weight.shape[1] // (2 * head_size)
    per_kv = local_heads // local_kv
    query_rows = per_kv * token_count
    req_count = lax.axis_size("req")
    req_index = lax.axis_index("req")
    tp_index = lax.axis_index("tp")
    cache_rows = prefix_cache.shape[0]
    prefix_len = cache_rows * req_count // 2
    score_scale = head_size ** (-0.5)
    full_rows = lax.all_gather(hidden_states, "tp", axis=1, tiled=True)
    normed_attn = rms_rows(full_rows, attn_gain)
    positions = (prefix_len + jnp.arange(token_count, dtype=jnp.int32)).astype(jnp.float32)
    queries = jnp.dot(normed_attn, query_weight, preferred_element_type=jnp.float32)
    fresh = jnp.dot(normed_attn, key_value_weight, preferred_element_type=jnp.float32).reshape(
        token_count, local_kv, 2, head_size
    )
    queries = rotate(queries.reshape(token_count, local_heads, head_size), positions).astype(
        jnp.bfloat16
    )
    new_keys = rotate(fresh[:, :, 0], positions).astype(jnp.bfloat16)
    new_values = fresh[:, :, 1].astype(jnp.bfloat16)
    query_heads = (
        queries.reshape(token_count, local_kv, per_kv, head_size)
        .transpose(1, 2, 0, 3)
        .reshape(local_kv, query_rows, head_size)
    )

    def absorb(carried, key_rows, value_rows, keep_mask):
        peak, denominator, accum = carried
        scores = (
            jnp.einsum("hqd,khd->hqk", query_heads, key_rows, preferred_element_type=jnp.float32)
            * score_scale
        )
        scores = jnp.where(keep_mask, scores, -jnp.inf)
        new_peak = jnp.maximum(peak, jnp.max(scores, axis=-1))
        weights = jnp.exp(scores - new_peak[..., None])
        decay_old = jnp.exp(peak - new_peak)
        denominator = denominator * decay_old + jnp.sum(weights, axis=-1)
        accum = accum * decay_old[..., None] + jnp.einsum(
            "hqk,khd->hqd",
            weights.astype(jnp.bfloat16),
            value_rows,
            preferred_element_type=jnp.float32,
        )
        return (new_peak, denominator, accum)

    sink_rows = jnp.broadcast_to(
        sink_logits.reshape(local_kv, per_kv, 1), (local_kv, per_kv, token_count)
    ).reshape(local_kv, query_rows)
    running = (
        sink_rows,
        jnp.ones_like(sink_rows),
        jnp.zeros((local_kv, query_rows, head_size), jnp.float32),
    )
    row_pos = jnp.arange(query_rows, dtype=jnp.int32) % token_count
    causal = jnp.arange(token_count, dtype=jnp.int32)[None, :] <= row_pos[:, None]
    running = absorb(running, new_keys, new_values, causal)
    own_group = prefix_group[req_index]
    shard_rows = lax.all_gather(prefix_cache, "req", axis=0, tiled=True)
    row_total = shard_rows.shape[0]
    block_rows = 512
    block_data = shard_rows.reshape(row_total // block_rows, block_rows, local_kv, 2, head_size)

    def one_block(current, scan_item):
        number, block_keys = scan_item
        keep_rows = (
            number * block_rows + jnp.arange(block_rows, dtype=jnp.int32)
        ) // prefix_len == own_group

        def include(state_in):
            return absorb(
                state_in, block_keys[:, :, 0], block_keys[:, :, 1], keep_rows[None, None, :]
            )

        def unchanged(state_in):
            return state_in

        return (lax.cond(jnp.any(keep_rows), include, unchanged, current), None)

    result_state, unused_out = lax.scan(
        one_block, running, (jnp.arange(row_total // block_rows, dtype=jnp.int32), block_data)
    )
    running = result_state
    final_peak, final_denominator, final_accum = running
    mixed = (final_accum / final_denominator[..., None]).astype(jnp.bfloat16)
    mixed = (
        mixed.reshape(local_kv, per_kv, token_count, head_size)
        .transpose(2, 0, 1, 3)
        .reshape(token_count, local_heads * head_size)
    )
    attn_part = jnp.dot(mixed, out_weight, preferred_element_type=jnp.float32)
    attn_sum = lax.psum_scatter(attn_part, "tp", scatter_dimension=1, tiled=True)
    col_count = attn_sum.shape[1]
    live = (jnp.arange(token_count, dtype=jnp.int32) < suffix_lengths[req_index])[:, None]
    attn_out = jnp.where(live, attn_sum, 0.0).astype(jnp.bfloat16)
    resid = (hidden_states.astype(jnp.float32) + attn_sum).astype(jnp.bfloat16)
    expert_count = router_weight.shape[1]
    top_count = route_ids.shape[1]
    capacity = token_count * top_count * 3 // (2 * expert_count)
    entries = route_ids.reshape(-1)
    onehot = (entries[:, None] == jnp.arange(expert_count, dtype=jnp.int32)[None, :]).astype(
        jnp.int32
    )
    earlier = jnp.cumsum(onehot, axis=0) - onehot
    slots = jnp.sum(earlier * onehot, axis=1)
    targets = entries * capacity + slots
    sources = jnp.arange(token_count * top_count, dtype=jnp.int32) // top_count
    source_of = jnp.zeros((expert_count * capacity,), jnp.int32).at[targets].set(sources)
    filled = jnp.zeros((expert_count * capacity,), jnp.bool_).at[targets].set(True)
    exp_local = gate_up_weight.shape[0]
    ff_local = gate_up_weight.shape[3]
    joined_weight = gate_up_weight.reshape(exp_local, model_width, 2 * ff_local)
    resid_rows = lax.all_gather(resid, "tp", axis=1, tiled=True)
    normed_rows = rms_rows(resid_rows, ffn_gain)
    normed_part = lax.dynamic_slice_in_dim(normed_rows, tp_index * col_count, col_count, 1)
    picked_rows = jnp.where(filled[:, None], normed_rows[source_of], jnp.zeros((), jnp.bfloat16))
    arrived = lax.all_to_all(
        picked_rows.reshape(expert_count, capacity, normed_rows.shape[1]),
        "req",
        split_axis=0,
        concat_axis=0,
        tiled=True,
    )
    item_count = arrived.shape[1]
    grouped = arrived.reshape(req_count, exp_local, item_count, model_width)
    projected = jnp.einsum(
        "sepd,edf->sepf", grouped, joined_weight, preferred_element_type=jnp.float32
    )
    gate_value = jnp.minimum(projected[..., :ff_local], clamp_limit)
    up_value = jnp.clip(projected[..., ff_local:], -clamp_limit, clamp_limit)
    active = ((up_value + 1.0) * gate_value * jax.nn.sigmoid(glu_alpha * gate_value)).astype(
        jnp.bfloat16
    )
    results = jnp.einsum(
        "sepf,efd->sepd", active, down_weight, preferred_element_type=jnp.float32
    ).astype(jnp.bfloat16)
    send_results = results.reshape(arrived.shape[0], item_count, model_width)
    returned = lax.all_to_all(send_results, "req", split_axis=0, concat_axis=0, tiled=True)
    logits = lax.psum(jnp.dot(normed_part, router_weight, preferred_element_type=jnp.float32), "tp")
    chosen = jnp.take_along_axis(logits, route_ids, axis=1)
    raised = jnp.exp(chosen)
    gates = raised / jnp.sum(raised, axis=1, keepdims=True)
    picked_back = returned.reshape(expert_count * capacity, model_width)[targets]
    combined = jnp.sum(
        picked_back.reshape(token_count, top_count, model_width).astype(jnp.float32)
        * gates[:, :, None],
        axis=1,
    )
    moe_sum = lax.psum_scatter(combined, "tp", scatter_dimension=1, tiled=True)
    moe_out = jnp.where(live, moe_sum, 0.0).astype(jnp.bfloat16)
    return (attn_out, moe_out)


def solution(mesh):
    return jax.shard_map(
        local,
        mesh=mesh,
        in_specs=(
            P("req", "tp"),
            P(),
            P(None, "tp"),
            P(None, "tp"),
            P("tp"),
            P("req", "tp"),
            P("tp", None),
            P(),
            P("tp", None),
            P("req", None, None, "tp"),
            P("req", "tp", None),
            P("req", None),
            P(),
            P(),
        ),
        out_specs=(P("req", "tp"), P("req", "tp")),
        check_vma=False,
    )
```

profile of v0, /device:TPU:8, one launch (start us, length us, event | category | flops | bytes accessed | tf_op | source)
XLA Modules:
  0.0 859.6 jit_solution(3098515583077833532)
XLA Ops:
  8.0 32.7 %all_gather.9 = bf16[128,2880]{0,1:T(8,128)(2,1)S(1)} all-gather(bf16[128,360]{0,1:T(8,128)(2,1)} %param.18), channel_id=1, replica_groups=mesh['req'=32,'tp'=8] {'tp'}, dimensions={1}, use_global_device_ids=true | all-gather | bytes 829440 | tf_op jit(solution)/shard_map/all_gather | solution.py:68
  41.2 3.5 fusion.40
  48.9 43.1 %all-gather.2.cloned.1.call-done = bf16[32768,128]{1,0:T(8,128)(2,1)} async-done(((bf16[1024,128]{1,0:T(8,128)(2,1)}), bf16[32768,128]{1,0:T(8,128)(2,1)}) %all-gather.2.cloned.1.call-update) | async-done | bytes 8388624 | tf_op jit(solution)/shard_map/all_gather | solution.py:117
  92.0 27.8 %reshape.537 = bf16[64,512,1,2,64]{4,3,1,0,2:T(2,128)(2,1)} reshape(bf16[32768,128]{1,0:T(8,128)(2,1)} %all-gather.2.cloned.1.call-done) | data formatting | bytes 16777216 | tf_op jit(solution)/shard_map/reshape | solution.py:120
  119.8 33.3 %copy.91 = bf16[64,512,1,2,64]{1,4,3,2,0:T(8,128)(2,1)} copy(bf16[64,512,1,2,64]{4,3,1,0,2:T(2,128)(2,1)} %reshape.537) | data formatting | bytes 16777216 | tf_op jit(solution)/shard_map/while | solution.py:138
  153.2 286.7 %while.16 = (s32[]{:T(128)}, f32[1,1024]{1,0:T(1,128)S(1)}, f32[1,1024]{1,0:T(1,128)S(1)}, f32[1,1024,64]{1,2,0:T(8,128)S(1)}, s32[64]{0:T(128)S(1)}, /*index=5*...) while((s32[]{:T(128)}, f32[1,1024]{1,0:T(1,128)S(1)}, ...), condition=%wide.region_9.10_spmd, body=%wide.region_3.9_spmd.sunk | while | flops 140127232 | bytes 7538951 | solution.py:138
  197.0 2.7 conditional.2
  243.6 2.7 conditional.2
  255.3 2.7 conditional.2
  449.5 34.8 %reduce-scatter.9.cloned.1.call-done = f32[128,360]{0,1:T(8,128)} async-done(((f32[128,2880]{0,1:T(8,128)}), f32[128,360]{0,1:T(8,128)}) %reduce-scatter.9.cloned.1.call-update) | async-done | bytes 184336
  485.2 29.5 %all_gather.11 = bf16[128,2880]{0,1:T(8,128)(2,1)S(1)} all-gather(bf16[128,360]{0,1:T(8,128)(2,1)S(1)} %add_convert_fusion), channel_id=1, replica_groups=mesh['req'=32,'tp'=8] {'tp'}, dimensions={1}, use_global_device_ids=true | all-gather | bytes 829440 | tf_op jit(solution)/shard_map/all_gather | solution.py:171
  515.6 4.9 gather_fusion
  520.4 2.8 broadcast_select_fusion
  523.2 96.6 %all_to_all.10 = bf16[32,24,2880]{2,1,0:T(8,128)(2,1)S(1)} all-to-all(bf16[32,24,2880]{2,1,0:T(8,128)(2,1)S(1)} %broadcast_select_fusion), channel_id=1, replica_groups=mesh['req'=32,'tp'=8] {'req'}, dimensions={0} | all-to-all | bytes 8847360 | tf_op jit(solution)/shard_map/all_to_all | solution.py:175
  619.8 6.2 convolution_bitcast_fusion.1
  626.0 4.6 convolution_convert_fusion
  630.6 21.0 %all-to-all-start.1 = ((bf16[32,24,2880]{2,1,0:T(8,128)(2,1)}), bf16[32,24,2880]{2,1,0:T(8,128)(2,1)}, u32[]{:S(2)}, u32[]{:S(2)}) async-start(bf16[32,24,2880]{2,1,0:T(8,128)(2,1)} %convolution_convert_fusion), calls=%async_computation.1 | async-start | bytes 9043968 | tf_op jit(solution)/shard_map/all_to_all | solution.py:196
  652.1 123.0 %psum.7 = f32[128,32]{0,1:T(8,128)S(1)} all-reduce(f32[128,32]{0,1:T(8,128)S(1)} %fusion.45), channel_id=1, replica_groups=mesh['req'=32,'tp'=8] {'tp'}, use_global_device_ids=true, to_apply=%region_17.18 | all-reduce | flops 4096 | bytes 32768 | tf_op jit(solution)/shard_map/psum | solution.py:197
  775.1 3.7 gather_fusion.2
  779.2 9.7 %gather_fusion.1 = bf16[512,2880]{1,0:T(8,128)(2,1)} fusion(bf16[768,2880]{1,0:T(8,128)(2,1)} %bitcast.44, s32[1024]{0:T(1024)S(1)} %pad_clamp_fusion), kind=kCustom, calls=%fused_computation.1 | custom fusion | bytes 5900288 | tf_op jit(solution)/shard_map/gather | solution.py:201
  788.9 6.5 reshape.490
  795.4 8.3 multiply_reduce_fusion
  803.7 3.0 copy.102
  808.0 43.5 %reduce-scatter.11.cloned.1.call-done = f32[128,360]{0,1:T(8,128)} async-done(((f32[128,2880]{0,1:T(8,128)}), f32[128,360]{0,1:T(8,128)}) %reduce-scatter.11.cloned.1.call-update) | async-done | bytes 184336
  (509 shorter events, 304.7 us)
Async XLA Ops:
  7.2 432.8 %copy-start = (bf16[512,2880]{0,1:T(8,128)(2,1)S(1)}, bf16[512,2880]{0,1:T(8,128)(2,1)}, u32[]{:S(2)}) copy-start(bf16[512,2880]{0,1:T(8,128)(2,1)} %param.24) | copy-start | bytes 8847364
  7.2 84.8 %all-gather.2.cloned.1.call-start = ((), (), s32[]{:S(2)}) async-start(), calls=%async_computation.4 | async-start | bytes 8650752 | tf_op jit(solution)/shard_map/all_gather | solution.py:117
  7.9 476.3 %reduce-scatter.9.cloned.1.call-start = ((), (), s32[]{:S(2)}) async-start(), calls=%async_computation.5 | async-start | bytes 1658880
  40.7 4.1 copy-start.2
  41.2 3.9 copy-start.11
  41.2 4.5 copy-start.10
  44.8 3.6 copy-start.8
  440.0 2.1 copy-start.5
  442.1 42.2 %copy-start.4 = (bf16[128,360]{0,1:T(8,128)(2,1)S(1)}, bf16[128,360]{0,1:T(8,128)(2,1)}, u32[]{:S(2)}) copy-start(bf16[128,360]{0,1:T(8,128)(2,1)} %param.18) | copy-start | bytes 276484
  442.1 73.2 %copy-start.7 = (f32[2880]{0:T(1024)S(1)}, f32[2880]{0:T(1024)}, u32[]{:S(2)}) copy-start(f32[2880]{0:T(1024)} %param.25) | copy-start | bytes 34564
  619.8 6.2 copy-start.9
  630.6 21.3 %copy-start.6 = (bf16[360,32]{0,1:T(8,128)(2,1)S(1)}, bf16[360,32]{0,1:T(8,128)(2,1)}, u32[]{:S(2)}) copy-start(bf16[360,32]{0,1:T(8,128)(2,1)} %param.26) | copy-start | bytes 69124
  630.6 148.6 %all-to-all-start.1 = ((bf16[32,24,2880]{2,1,0:T(8,128)(2,1)}), bf16[32,24,2880]{2,1,0:T(8,128)(2,1)}, u32[]{:S(2)}, u32[]{:S(2)}) async-start(bf16[32,24,2880]{2,1,0:T(8,128)(2,1)} %convolution_convert_fusion), calls=%async_computation.1 | async-start | bytes 9043968 | tf_op jit(solution)/shard_map/all_to_all | solution.py:196
  651.6 199.9 %reduce-scatter.11.cloned.1.call-start = ((), (), s32[]{:S(2)}) async-start(), calls=%async_computation.6 | async-start | bytes 1658880
  795.4 57.7 %copy-start.1 = (bf16[512,2880]{0,1:T(8,128)(2,1)S(1)}, bf16[512,2880]{0,1:T(8,128)(2,1)}, u32[]{:S(2)}) copy-start(bf16[512,2880]{0,1:T(8,128)(2,1)} %param.24) | copy-start | bytes 8847364
  803.7 3.0 copy-start.12
  803.7 47.7 %copy-start.3 = (f32[128,360]{0,1:T(8,128)S(1)}, f32[128,360]{0,1:T(8,128)}, u32[]{:S(2)}) copy-start(f32[128,360]{0,1:T(8,128)} %reduce-scatter.9.cloned.1.call-done) | copy-start | bytes 552964
Sparse Core Ops, SparseCore 0:
  10.6 81.3 all-gather.1
  442.2 41.9 reduce-scatter.8
  806.9 44.5 reduce-scatter.10
where the time goes:
time: 864 us; the launch traced here: 860 us
  blocking collectives  282 us (33%)
  local copies, waits for them, and re-layouts  166 us (19%)
  waiting for transfers between devices  122 us (14%)
  other arithmetic  116 us (13%)
  loops' own time  81 us (9%)
  matrix products  57.6 us (7%)
  starting transfers between devices  21.1 us (2%)
  between operations  14.2 us (2%)
    psum x1, blocking collectives, local(): lax.psum(jnp.dot(normed_part, router_weight, preferred_element_type=jnp.f...  123 us
    all_to_all x1, blocking collectives, local(): lax.all_to_all(picked_rows.reshape(expert_count, capacity, normed_rows.sh...  96.6 us
    reduce_or x64, other arithmetic, one_block(): return (lax.cond(jnp.any(keep_rows), include, unchanged, current), None)  82 us
    unnamed x5, waiting for transfers between devices  78.9 us
    another operation x1, loops' own time, local(): lax.scan(one_block, running, (jnp.arange(row_total // block_rows, dtype=j...  78.7 us
    all_gather x1, waiting for transfers between devices, local(): shard_rows = lax.all_gather(prefix_cache, 'req', axis=0, tiled=True)  43.1 us
    dynamic_slice x64, local copies, waits for them, and re-layouts, local(): lax.scan(one_block, running, (jnp.arange(row_total // block_rows, dtype=j...  39.2 us
    while x2, local copies, waits for them, and re-layouts, local(): lax.scan(one_block, running, (jnp.arange(row_total // block_rows, dtype=j...  33.5 us
  transfers between devices with their start and end apart: 4, of which 3 were waited for; matrix products, arithmetic and copies ran while one was open for 2% of the time, Pallas kernels for 0%

commit v1 on v0

--- a/solution.py
+++ b/solution.py
@@ -1,6 +1,10 @@
+import functools
+
 import jax
 import jax.numpy as jnp
 from jax import lax
+from jax.experimental import pallas as pl
+from jax.experimental.pallas import tpu as pltpu
 from jax.sharding import PartitionSpec as P
 
 D = 2880
@@ -34,6 +38,73 @@
         ],
         axis=-1,
     )
+
+
+def flash_kernel(group_ref, q_ref, kv_ref, m0_ref, l0_ref, acc0_ref, out_ref, m_sc, l_sc, acc_sc, *, scale, steps):
+    step = pl.program_id(1)
+
+    @pl.when(step == 0)
+    def _():
+        m_sc[...] = m0_ref[...]
+        l_sc[...] = l0_ref[...]
+        acc_sc[...] = acc0_ref[...]
+
+    block = kv_ref[...]
+    scores = (
+        lax.dot_general(
+            q_ref[...], block, (((1,), (1,)), ((), ())), preferred_element_type=jnp.float32
+        )
+        * scale
+    )
+    m_prev = m_sc[...]
+    m_new = jnp.maximum(m_prev, jnp.max(scores, axis=1, keepdims=True))
+    weights = jnp.exp(scores - m_new)
+    decay = jnp.exp(m_prev - m_new)
+    l_sc[...] = decay * l_sc[...] + jnp.sum(weights, axis=1, keepdims=True)
+    acc_sc[...] = decay * acc_sc[...] + jnp.dot(
+        weights.astype(jnp.bfloat16), block, preferred_element_type=jnp.float32
+    )
+    m_sc[...] = m_new
+
+    @pl.when(step == steps - 1)
+    def _():
+        out_ref[...] = (acc_sc[...] / l_sc[...]).astype(out_ref.dtype)
+
+
+def prefix_attention(group, query, cache, peak, denominator, accum, *, prefix_len, scale):
+    rows, width = query.shape
+    block_q = min(rows, 1024)
+    block_k = 1024
+    steps = prefix_len // block_k
+    grid = (rows // block_q, steps)
+    kernel = functools.partial(flash_kernel, scale=scale, steps=steps)
+    return pl.pallas_call(
+        kernel,
+        out_shape=jax.ShapeDtypeStruct((rows, width), jnp.bfloat16),
+        grid_spec=pltpu.PrefetchScalarGridSpec(
+            num_scalar_prefetch=1,
+            grid=grid,
+            in_specs=[
+                pl.BlockSpec((block_q, width), lambda i, j, g: (i, 0)),
+                pl.BlockSpec((block_k, width), lambda i, j, g: (g[0] * steps + j, 0)),
+                pl.BlockSpec((block_q, 1), lambda i, j, g: (i, 0)),
+                pl.BlockSpec((block_q, 1), lambda i, j, g: (i, 0)),
+                pl.BlockSpec((block_q, width), lambda i, j, g: (i, 0)),
+            ],
+            out_specs=pl.BlockSpec((block_q, width), lambda i, j, g: (i, 0)),
+            scratch_shapes=[
+                pltpu.VMEM((block_q, 1), jnp.float32),
+                pltpu.VMEM((block_q, 1), jnp.float32),
+                pltpu.VMEM((block_q, width), jnp.float32),
+            ],
+        ),
+        compiler_params=pltpu.CompilerParams(dimension_semantics=("arbitrary", "arbitrary")),
+        cost_estimate=pl.CostEstimate(
+            flops=4 * rows * prefix_len * width,
+            transcendentals=rows * prefix_len,
+            bytes_accessed=prefix_len * width * 2 + rows * width * 8,
+        ),
+    )(group, query, cache, peak, denominator, accum)
 
 
 def local(
@@ -65,6 +136,7 @@
     cache_rows = prefix_cache.shape[0]
     prefix_len = cache_rows * req_count // 2
     score_scale = head_size ** (-0.5)
+    router_full = lax.all_gather(router_weight, "tp", axis=0, tiled=True)
     full_rows = lax.all_gather(hidden_states, "tp", axis=1, tiled=True)
     normed_attn = rms_rows(full_rows, attn_gain)
     positions = (prefix_len + jnp.arange(token_count, dtype=jnp.int32)).astype(jnp.float32)
@@ -82,71 +154,40 @@
         .transpose(1, 2, 0, 3)
         .reshape(local_kv, query_rows, head_size)
     )
-
-    def absorb(carried, key_rows, value_rows, keep_mask):
-        peak, denominator, accum = carried
-        scores = (
-            jnp.einsum("hqd,khd->hqk", query_heads, key_rows, preferred_element_type=jnp.float32)
-            * score_scale
-        )
-        scores = jnp.where(keep_mask, scores, -jnp.inf)
-        new_peak = jnp.maximum(peak, jnp.max(scores, axis=-1))
-        weights = jnp.exp(scores - new_peak[..., None])
-        decay_old = jnp.exp(peak - new_peak)
-        denominator = denominator * decay_old + jnp.sum(weights, axis=-1)
-        accum = accum * decay_old[..., None] + jnp.einsum(
-            "hqk,khd->hqd",
-            weights.astype(jnp.bfloat16),
-            value_rows,
-            preferred_element_type=jnp.float32,
-        )
-        return (new_peak, denominator, accum)
-
+    assert local_kv == 1
+    query_flat = query_heads.reshape(query_rows, head_size)
+    fresh_kv = jnp.concatenate([new_keys[:, 0, :], new_values[:, 0, :]], axis=1)
     sink_rows = jnp.broadcast_to(
-        sink_logits.reshape(local_kv, per_kv, 1), (local_kv, per_kv, token_count)
-    ).reshape(local_kv, query_rows)
-    running = (
-        sink_rows,
-        jnp.ones_like(sink_rows),
-        jnp.zeros((local_kv, query_rows, head_size), jnp.float32),
-    )
+        sink_logits.reshape(per_kv, 1), (per_kv, token_count)
+    ).reshape(query_rows, 1)
     row_pos = jnp.arange(query_rows, dtype=jnp.int32) % token_count
     causal = jnp.arange(token_count, dtype=jnp.int32)[None, :] <= row_pos[:, None]
-    running = absorb(running, new_keys, new_values, causal)
-    own_group = prefix_group[req_index]
+    fresh_scores = (
+        jnp.dot(query_flat, new_keys[:, 0, :].T, preferred_element_type=jnp.float32) * score_scale
+    )
+    fresh_scores = jnp.where(causal, fresh_scores, -jnp.inf)
+    start_peak = jnp.maximum(sink_rows, jnp.max(fresh_scores, axis=1, keepdims=True))
+    fresh_weights = jnp.exp(fresh_scores - start_peak)
+    start_denominator = jnp.exp(sink_rows - start_peak) + jnp.sum(
+        fresh_weights, axis=1, keepdims=True
+    )
+    start_accum = jnp.dot(
+        fresh_weights.astype(jnp.bfloat16), fresh_kv, preferred_element_type=jnp.float32
+    )
+    query_padded = jnp.concatenate([query_flat, jnp.zeros_like(query_flat)], axis=1)
+    own_group = prefix_group[req_index].reshape(1)
     shard_rows = lax.all_gather(prefix_cache, "req", axis=0, tiled=True)
-    row_total = shard_rows.shape[0]
-    block_rows = 512
-    block_data = shard_rows.reshape(row_total // block_rows, block_rows, local_kv, 2, head_size)
-
-    def one_block(current, scan_item):
-        number, block_keys = scan_item
-        keep_rows = (
-            number * block_rows + jnp.arange(block_rows, dtype=jnp.int32)
-        ) // prefix_len == own_group
-
-        def include(state_in):
-            return absorb(
-                state_in, block_keys[:, :, 0], block_keys[:, :, 1], keep_rows[None, None, :]
-            )
-
-        def unchanged(state_in):
-            return state_in
-
-        return (lax.cond(jnp.any(keep_rows), include, unchanged, current), None)
-
-    result_state, unused_out = lax.scan(
-        one_block, running, (jnp.arange(row_total // block_rows, dtype=jnp.int32), block_data)
-    )
-    running = result_state
-    final_peak, final_denominator, final_accum = running
-    mixed = (final_accum / final_denominator[..., None]).astype(jnp.bfloat16)
-    mixed = (
-        mixed.reshape(local_kv, per_kv, token_count, head_size)
-        .transpose(2, 0, 1, 3)
-        .reshape(token_count, local_heads * head_size)
-    )
-    attn_part = jnp.dot(mixed, out_weight, preferred_element_type=jnp.float32)
+    mixed_wide = prefix_attention(
+        own_group, query_padded, shard_rows, start_peak, start_denominator, start_accum,
+        prefix_len=prefix_len, scale=score_scale,
+    )
+    mixed = mixed_wide[:, head_size:].reshape(local_heads, token_count, head_size)
+    attn_part = jnp.einsum(
+        "hqd,hdo->qo",
+        mixed,
+        out_weight.reshape(local_heads, head_size, model_width),
+        preferred_element_type=jnp.float32,
+    )
     attn_sum = lax.psum_scatter(attn_part, "tp", scatter_dimension=1, tiled=True)
     col_count = attn_sum.shape[1]
     live = (jnp.arange(token_count, dtype=jnp.int32) < suffix_lengths[req_index])[:, None]
@@ -170,7 +211,6 @@
     joined_weight = gate_up_weight.reshape(exp_local, model_width, 2 * ff_local)
     resid_rows = lax.all_gather(resid, "tp", axis=1, tiled=True)
     normed_rows = rms_rows(resid_rows, ffn_gain)
-    normed_part = lax.dynamic_slice_in_dim(normed_rows, tp_index * col_count, col_count, 1)
     picked_rows = jnp.where(filled[:, None], normed_rows[source_of], jnp.zeros((), jnp.bfloat16))
     arrived = lax.all_to_all(
         picked_rows.reshape(expert_count, capacity, normed_rows.shape[1]),
@@ -194,7 +234,7 @@
     ).astype(jnp.bfloat16)
     send_results = results.reshape(arrived.shape[0], item_count, model_width)
     returned = lax.all_to_all(send_results, "req", split_axis=0, concat_axis=0, tiled=True)
-    logits = lax.psum(jnp.dot(normed_part, router_weight, preferred_element_type=jnp.float32), "tp")
+    logits = jnp.dot(normed_rows, router_full, preferred_element_type=jnp.float32)
     chosen = jnp.take_along_axis(logits, route_ids, axis=1)
     raised = jnp.exp(chosen)
     gates = raised / jnp.sum(raised, axis=1, keepdims=True)

time: 864 us -> 560 us (0.65)
  local copies, waits for them, and re-layouts: 166 us -> 43.7 us
  other arithmetic: 116 us -> 18 us
  loops' own time: 81 us -> 0 us
  Pallas kernels: 0 us -> 45.3 us
  matrix products: 57.6 us -> 22.4 us
    psum x1 -> x0, blocking collectives: 123 us -> none  [local(): lax.psum(jnp.dot(normed_part, router_weight, preferred_element_type=jnp.f...]
    all_gather x0 -> x1, blocking collectives: none -> 122 us  [local(): router_full = lax.all_gather(router_weight, 'tp', axis=0, tiled=True)]
    reduce_or x64 -> x0, other arithmetic: 82 us -> none  [one_block(): return (lax.cond(jnp.any(keep_rows), include, unchanged, current), None)]
    another operation x65 -> x0, loops' own time: 81 us -> none  [the longest x1 78.7 us: local(): lax.scan(one_block, running, (jnp.arange(row_total // block_rows, dtype=j...]
    pallas_call x0 -> x1, Pallas kernels: none -> 45.3 us  [prefix_attention(): pl.pallas_call(kernel, out_shape=jax.ShapeDtypeStruct((rows, width), jnp....]
    dynamic_slice x65 -> x1, local copies, waits for them, and re-layouts: 39.8 us -> 0.58 us  [local(): own_group = prefix_group[req_index].reshape(1)]
    dot_general x68 -> x4, matrix products: 41.2 us -> 7.08 us  [the longest x1 5.39 us: local(): jnp.einsum('hqd,hdo->qo', mixed, out_weight.reshape(local_heads, head_siz...]
    while x2 -> x0, local copies, waits for them, and re-layouts: 33.5 us -> none  [local(): lax.scan(one_block, running, (jnp.arange(row_total // block_rows, dtype=j...]
  transfers between devices with their start and end apart: 4 -> 4, of which waited for: 3 -> 3; matrix products, arithmetic and copies ran while one was open for 2% -> 5% of each run, Pallas kernels for 0% -> 0%
where the time goes in v1:
time: 560 us; the launch traced here: 559 us
  blocking collectives  281 us (50%)
  waiting for transfers between devices  114 us (20%)
  Pallas kernels  45.3 us (8%)
  local copies, waits for them, and re-layouts  43.7 us (8%)
  matrix products  22.4 us (4%)
  starting transfers between devices  21.1 us (4%)
  other arithmetic  18 us (3%)
  between operations  14.2 us (3%)
    all_gather x1, blocking collectives, local(): router_full = lax.all_gather(router_weight, 'tp', axis=0, tiled=True)  122 us
    all_to_all x1, blocking collectives, local(): lax.all_to_all(picked_rows.reshape(expert_count, capacity, normed_rows.sh...  96.4 us
    unnamed x5, waiting for transfers between devices  77.2 us
    pallas_call x1, Pallas kernels, prefix_attention(): pl.pallas_call(kernel, out_shape=jax.ShapeDtypeStruct((rows, width), jnp....  45.3 us
    all_gather x1, waiting for transfers between devices, local(): shard_rows = lax.all_gather(prefix_cache, 'req', axis=0, tiled=True)  36.5 us
    all_gather x1, blocking collectives, local(): full_rows = lax.all_gather(hidden_states, 'tp', axis=1, tiled=True)  32.7 us
    all_gather x1, blocking collectives, local(): resid_rows = lax.all_gather(resid, 'tp', axis=1, tiled=True)  29.5 us
    all_to_all x1, starting transfers between devices, local(): lax.all_to_all(send_results, 'req', split_axis=0, concat_axis=0, tiled=True)  21 us
  transfers between devices with their start and end apart: 4, of which 3 were waited for; matrix products, arithmetic and copies ran while one was open for 5% of the time, Pallas kernels for 0%

profile of v1, /device:TPU:8, one launch (start us, length us, event | category | flops | bytes accessed | tf_op | source)
XLA Modules:
  0.0 559.3 jit_solution(3956870911898074276)
XLA Ops:
  8.0 32.7 %all_gather.12 = bf16[128,2880]{0,1:T(8,128)(2,1)S(1)} all-gather(bf16[128,360]{0,1:T(8,128)(2,1)} %param.14), channel_id=1, replica_groups=mesh['req'=32,'tp'=8] {'tp'}, dimensions={1}, use_global_device_ids=true | all-gather | bytes 829440 | tf_op jit(solution)/shard_map/all_gather | solution.py:140
  41.2 2.4 fusion.24
  43.9 2.2 fusion.22
  48.4 4.6 copy.88
  55.6 36.5 %all-gather.3.cloned.1.call-done.kv_ref = bf16[32768,128]{1,0:T(8,128)(2,1)} async-done(((bf16[1024,128]{1,0:T(8,128)(2,1)}), bf16[32768,128]{1,0:T(8,128)(2,1)}) %all-gather.3.cloned.1.call-update) | async-done | bytes 8388624 | tf_op jit(solution)/shard_map/all_gather | solution.py:179
  92.0 45.3 %shard_map.149 = bf16[1024,128]{1,0:T(8,128)(2,1)} custom-call(s32[1]{0:T(128)} %dynamic_slice.7.group_ref, bf16[1024,128]{1,0:T(8,128)(2,1)} %concatenate.36.q_ref, bf16[32768,128]{1,0:T(8,128)(2,1)} %all-gather.3.cloned.1.call-done.kv_ref, f32[1024,1]{1,0:T(8,128)} %copy-done.3, f32[1024,1]{1,0:T(8,128)} %exponential_add_fusion.l0_ref, ...), custom_call_target="tpu_custom_call" | custom-call | flops 8589934592 | bytes 5242880 | tf_op jit(solution)/shard_map/pallas_call | solution.py:81
  138.4 5.4 convolution_bitcast_fusion
  146.0 2.6 scatter_custom_fusion.1
  148.7 2.4 scatter_custom_fusion
  151.2 34.8 %reduce-scatter.9.cloned.1.call-done = f32[128,360]{0,1:T(8,128)} async-done(((f32[128,2880]{0,1:T(8,128)}), f32[128,360]{0,1:T(8,128)}) %reduce-scatter.9.cloned.1.call-update) | async-done | bytes 184336
  186.9 29.5 %all_gather.14 = bf16[128,2880]{0,1:T(8,128)(2,1)S(1)} all-gather(bf16[128,360]{0,1:T(8,128)(2,1)S(1)} %add_convert_fusion), channel_id=1, replica_groups=mesh['req'=32,'tp'=8] {'tp'}, dimensions={1}, use_global_device_ids=true | all-gather | bytes 829440 | tf_op jit(solution)/shard_map/all_gather | solution.py:212
  217.3 4.9 gather_fusion
  222.2 2.8 broadcast_select_fusion
  224.9 96.4 %all_to_all.10 = bf16[32,24,2880]{2,1,0:T(8,128)(2,1)S(1)} all-to-all(bf16[32,24,2880]{2,1,0:T(8,128)(2,1)S(1)} %broadcast_select_fusion), channel_id=1, replica_groups=mesh['req'=32,'tp'=8] {'req'}, dimensions={0} | all-to-all | bytes 8847360 | tf_op jit(solution)/shard_map/all_to_all | solution.py:215
  321.3 6.2 %convolution_bitcast_fusion.1 = f32[32,1,24,720]{3,2,0,1:T(8,128)S(1)} fusion(bf16[32,24,2880]{2,1,0:T(8,128)(2,1)S(1)} %all_to_all.10, bf16[2880,720,1]{0,1,2:T(8,128)(2,1)} %bitcast.100), kind=kOutput, calls=%fused_computation.14 | convolution fusion | flops 3185049600 | bytes 10782720 | tf_op jit(solution)/shard_map/sepd,edf->sepf/dot_general | solution.py:224
  327.6 4.6 convolution_convert_fusion
  332.1 21.0 %all-to-all-start.1 = ((bf16[32,24,2880]{2,1,0:T(8,128)(2,1)}), bf16[32,24,2880]{2,1,0:T(8,128)(2,1)}, u32[]{:S(2)}, u32[]{:S(2)}) async-start(bf16[32,24,2880]{2,1,0:T(8,128)(2,1)} %convolution_convert_fusion), calls=%async_computation.1 | async-start | bytes 9043968 | tf_op jit(solution)/shard_map/all_to_all | solution.py:236
  353.2 122.4 %all-gather = bf16[8,360,32]{1,2,0:T(8,128)(2,1)S(1)} all-gather(bf16[1,360,32]{1,2,0:T(8,128)(2,1)S(1)} %bitcast.94), channel_id=1, replica_groups=mesh['req'=32,'tp'=8] {'tp'}, dimensions={0}, use_global_device_ids=true | all-gather | bytes 207360 | tf_op jit(solution)/shard_map/all_gather | solution.py:139
  476.5 3.8 gather_fusion.2
  480.6 9.7 %gather_fusion.1 = bf16[512,2880]{1,0:T(8,128)(2,1)} fusion(bf16[768,2880]{1,0:T(8,128)(2,1)} %bitcast.32, s32[1024]{0:T(1024)S(1)} %pad_clamp_fusion), kind=kCustom, calls=%fused_computation.1 | custom fusion | bytes 5900288 | tf_op jit(solution)/shard_map/gather | solution.py:241
  490.3 6.5 %reshape.378 = f32[128,4,2880]{2,1,0:T(4,128)} reshape(bf16[512,2880]{1,0:T(8,128)(2,1)} %gather_fusion.1) | data formatting | bytes 8847360 | tf_op jit(solution)/shard_map/convert_element_type | solution.py:243
  496.9 8.3 %multiply_reduce_fusion = f32[128,2880]{1,0:T(8,128)} fusion(f32[128,4,2880]{2,1,0:T(4,128)} %reshape.378, f32[128,4]{1,0:T(8,128)S(1)} %copy.98), kind=kLoop, calls=%fused_computation.5 | loop fusion | flops 2580480 | bytes 7374848 | tf_op jit(solution)/shard_map/reduce_sum | solution.py:242
  505.2 3.0 copy.99
  509.4 41.7 %reduce-scatter.11.cloned.1.call-done = f32[128,360]{0,1:T(8,128)} async-done(((f32[128,2880]{0,1:T(8,128)}), f32[128,360]{0,1:T(8,128)}) %reduce-scatter.11.cloned.1.call-update) | async-done | bytes 184336
  (98 shorter events, 15.5 us)
Async XLA Ops:
  7.2 34.1 %copy-start = (bf16[2880,512]{1,0:T(8,128)(2,1)S(1)}, bf16[2880,512]{1,0:T(8,128)(2,1)}, u32[]{:S(2)}) copy-start(bf16[2880,512]{1,0:T(8,128)(2,1)} %param.16) | copy-start | bytes 8847364
  7.2 84.9 %all-gather.3.cloned.1.call-start = ((), (), s32[]{:S(2)}) async-start(), calls=%async_computation.4 | async-start | bytes 8650752 | tf_op jit(solution)/shard_map/all_gather | solution.py:179
  7.9 178.1 %reduce-scatter.9.cloned.1.call-start = ((), (), s32[]{:S(2)}) async-start(), calls=%async_computation.5 | async-start | bytes 1658880
  40.7 3.0 copy-start.2
  41.2 2.7 copy-start.11
  43.7 3.0 copy-start.9
  47.6 7.2 %copy-start.3 = (f32[1024,1]{1,0:T(8,128)}, f32[1024,1]{1,0:T(8,128)S(1)}, u32[]{:S(2)}) copy-start(f32[1024,1]{1,0:T(8,128)S(1)} %copy.87.m0_ref) | copy-start | bytes 12292
  48.4 4.6 copy-start.12
  138.4 5.4 copy-start.6
  143.8 42.2 %copy-start.5 = (bf16[128,360]{0,1:T(8,128)(2,1)S(1)}, bf16[128,360]{0,1:T(8,128)(2,1)}, u32[]{:S(2)}) copy-start(bf16[128,360]{0,1:T(8,128)(2,1)} %param.14) | copy-start | bytes 276484
  143.9 73.2 %copy-start.8 = (f32[2880]{0:T(1024)S(1)}, f32[2880]{0:T(1024)}, u32[]{:S(2)}) copy-start(f32[2880]{0:T(1024)} %param.21) | copy-start | bytes 34564
  321.3 6.2 %copy-start.10 = (bf16[1,360,2880]{2,1,0:T(8,128)(2,1)S(1)}, bf16[1,360,2880]{2,1,0:T(8,128)(2,1)}, u32[]{:S(2)}) copy-start(bf16[1,360,2880]{2,1,0:T(8,128)(2,1)} %param.24) | copy-start | bytes 6220804
  332.1 21.1 %copy-start.7 = (bf16[360,32]{0,1:T(8,128)(2,1)S(1)}, bf16[360,32]{0,1:T(8,128)(2,1)}, u32[]{:S(2)}) copy-start(bf16[360,32]{0,1:T(8,128)(2,1)} %param.22) | copy-start | bytes 69124
  332.1 148.5 %all-to-all-start.1 = ((bf16[32,24,2880]{2,1,0:T(8,128)(2,1)}), bf16[32,24,2880]{2,1,0:T(8,128)(2,1)}, u32[]{:S(2)}, u32[]{:S(2)}) async-start(bf16[32,24,2880]{2,1,0:T(8,128)(2,1)} %convolution_convert_fusion), calls=%async_computation.1 | async-start | bytes 9043968 | tf_op jit(solution)/shard_map/all_to_all | solution.py:236
  353.2 198.0 %reduce-scatter.11.cloned.1.call-start = ((), (), s32[]{:S(2)}) async-start(), calls=%async_computation.6 | async-start | bytes 1658880
  496.9 55.9 %copy-start.1 = (bf16[2880,512]{1,0:T(8,128)(2,1)S(1)}, bf16[2880,512]{1,0:T(8,128)(2,1)}, u32[]{:S(2)}) copy-start(bf16[2880,512]{1,0:T(8,128)(2,1)} %param.16) | copy-start | bytes 8847364
  505.1 3.0 copy-start.13
  505.1 46.0 %copy-start.4 = (f32[128,360]{0,1:T(8,128)S(1)}, f32[128,360]{0,1:T(8,128)}, u32[]{:S(2)}) copy-start(f32[128,360]{0,1:T(8,128)} %reduce-scatter.9.cloned.1.call-done) | copy-start | bytes 552964
Sparse Core Ops, SparseCore 0:
  10.6 81.4 all-gather.2
  144.0 41.9 reduce-scatter.8
  508.3 42.8 reduce-scatter.10

commit v2 on v1

--- a/solution.py
+++ b/solution.py
@@ -40,7 +40,7 @@
     )
 
 
-def flash_kernel(group_ref, q_ref, kv_ref, m0_ref, l0_ref, acc0_ref, out_ref, m_sc, l_sc, acc_sc, *, scale, steps):
+def flash_kernel(group_ref, q_ref, kv_ref, m0_ref, l0_ref, acc0_ref, m_out, l_out, acc_out, m_sc, l_sc, acc_sc, *, scale, steps):
     step = pl.program_id(1)
 
     @pl.when(step == 0)
@@ -68,30 +68,38 @@
 
     @pl.when(step == steps - 1)
     def _():
-        out_ref[...] = (acc_sc[...] / l_sc[...]).astype(out_ref.dtype)
-
-
-def prefix_attention(group, query, cache, peak, denominator, accum, *, prefix_len, scale):
+        m_out[...] = m_sc[...]
+        l_out[...] = l_sc[...]
+        acc_out[...] = acc_sc[...]
+
+
+def prefix_attention(group, query, cache, peak, denominator, accum, *, group_rows, scale):
     rows, width = query.shape
     block_q = min(rows, 1024)
-    block_k = 1024
-    steps = prefix_len // block_k
+    block_k = min(group_rows, 1024)
+    steps = group_rows // block_k
     grid = (rows // block_q, steps)
     kernel = functools.partial(flash_kernel, scale=scale, steps=steps)
+    row_spec = pl.BlockSpec((block_q, 1), lambda i, j, g: (i, 0))
+    wide_spec = pl.BlockSpec((block_q, width), lambda i, j, g: (i, 0))
     return pl.pallas_call(
         kernel,
-        out_shape=jax.ShapeDtypeStruct((rows, width), jnp.bfloat16),
+        out_shape=(
+            jax.ShapeDtypeStruct((rows, 1), jnp.float32),
+            jax.ShapeDtypeStruct((rows, 1), jnp.float32),
+            jax.ShapeDtypeStruct((rows, width), jnp.float32),
+        ),
         grid_spec=pltpu.PrefetchScalarGridSpec(
             num_scalar_prefetch=1,
             grid=grid,
             in_specs=[
-                pl.BlockSpec((block_q, width), lambda i, j, g: (i, 0)),
+                wide_spec,
                 pl.BlockSpec((block_k, width), lambda i, j, g: (g[0] * steps + j, 0)),
-                pl.BlockSpec((block_q, 1), lambda i, j, g: (i, 0)),
-                pl.BlockSpec((block_q, 1), lambda i, j, g: (i, 0)),
-                pl.BlockSpec((block_q, width), lambda i, j, g: (i, 0)),
+                row_spec,
+                row_spec,
+                wide_spec,
             ],
-            out_specs=pl.BlockSpec((block_q, width), lambda i, j, g: (i, 0)),
+            out_specs=[row_spec, row_spec, wide_spec],
             scratch_shapes=[
                 pltpu.VMEM((block_q, 1), jnp.float32),
                 pltpu.VMEM((block_q, 1), jnp.float32),
@@ -100,9 +108,9 @@
         ),
         compiler_params=pltpu.CompilerParams(dimension_semantics=("arbitrary", "arbitrary")),
         cost_estimate=pl.CostEstimate(
-            flops=4 * rows * prefix_len * width,
-            transcendentals=rows * prefix_len,
-            bytes_accessed=prefix_len * width * 2 + rows * width * 8,
+            flops=4 * rows * group_rows * width,
+            transcendentals=rows * group_rows,
+            bytes_accessed=group_rows * width * 2 + rows * width * 10,
         ),
     )(group, query, cache, peak, denominator, accum)
 
@@ -136,8 +144,9 @@
     cache_rows = prefix_cache.shape[0]
     prefix_len = cache_rows * req_count // 2
     score_scale = head_size ** (-0.5)
+    full_rows = lax.all_gather(hidden_states.T, "tp", axis=0, tiled=True).T
     router_full = lax.all_gather(router_weight, "tp", axis=0, tiled=True)
-    full_rows = lax.all_gather(hidden_states, "tp", axis=1, tiled=True)
+    full_rows, router_full = lax.optimization_barrier((full_rows, router_full))
     normed_attn = rms_rows(full_rows, attn_gain)
     positions = (prefix_len + jnp.arange(token_count, dtype=jnp.int32)).astype(jnp.float32)
     queries = jnp.dot(normed_attn, query_weight, preferred_element_type=jnp.float32)
@@ -176,11 +185,19 @@
     )
     query_padded = jnp.concatenate([query_flat, jnp.zeros_like(query_flat)], axis=1)
     own_group = prefix_group[req_index].reshape(1)
-    shard_rows = lax.all_gather(prefix_cache, "req", axis=0, tiled=True)
-    mixed_wide = prefix_attention(
-        own_group, query_padded, shard_rows, start_peak, start_denominator, start_accum,
-        prefix_len=prefix_len, scale=score_scale,
-    )
+    chunks = 4
+    piece = cache_rows // chunks
+    state = (start_peak, start_denominator, start_accum)
+    for chunk in range(chunks):
+        shard_rows = lax.all_gather(
+            prefix_cache[chunk * piece:(chunk + 1) * piece], "req", axis=0, tiled=True
+        )
+        state = prefix_attention(
+            own_group, query_padded, shard_rows, *state,
+            group_rows=prefix_len // chunks, scale=score_scale,
+        )
+    final_peak, final_denominator, final_accum = state
+    mixed_wide = (final_accum / final_denominator).astype(jnp.bfloat16)
     mixed = mixed_wide[:, head_size:].reshape(local_heads, token_count, head_size)
     attn_part = jnp.einsum(
         "hqd,hdo->qo",
@@ -209,7 +226,7 @@
     exp_local = gate_up_weight.shape[0]
     ff_local = gate_up_weight.shape[3]
     joined_weight = gate_up_weight.reshape(exp_local, model_width, 2 * ff_local)
-    resid_rows = lax.all_gather(resid, "tp", axis=1, tiled=True)
+    resid_rows = lax.all_gather(resid.T, "tp", axis=0, tiled=True).T
     normed_rows = rms_rows(resid_rows, ffn_gain)
     picked_rows = jnp.where(filled[:, None], normed_rows[source_of], jnp.zeros((), jnp.bfloat16))
     arrived = lax.all_to_all(

time: 560 us -> 653 us (1.17); the launches traced: 559 us -> 642 us
  waiting for transfers between devices: 114 us -> 273 us
  blocking collectives: 281 us -> 193 us
  Pallas kernels: 45.3 us -> 56.6 us
    all_to_all x1, waiting for transfers between devices: 0.01 us -> 98.6 us  [local(): lax.all_to_all(send_results, 'req', split_axis=0, concat_axis=0, tiled=True)]
    all_gather x1, blocking collectives: 122 us -> 29.3 us  [local(): router_full = lax.all_gather(router_weight, 'tp', axis=0, tiled=True)]
    all_gather x1 -> x4, waiting for transfers between devices: 36.5 us -> 99.4 us  [local(): lax.all_gather(prefix_cache[chunk * piece:(chunk + 1) * piece], 'req', ax...]
    pallas_call x1 -> x4, Pallas kernels: 45.3 us -> 56.6 us  [prefix_attention(): pl.pallas_call(kernel, out_shape=(jax.ShapeDtypeStruct((rows, 1), jnp.flo...]
    unnamed x5 -> x8, waiting for transfers between devices: 77.2 us -> 75 us
  transfers between devices with their start and end apart: 4 -> 7, of which waited for: 3 -> 6; matrix products, arithmetic and copies ran while one was open for 5% -> 5% of each run, Pallas kernels for 0% -> 7%
where the time goes in v2:
time: 653 us; the launch traced here: 642 us
  waiting for transfers between devices  273 us (42%)
  blocking collectives  193 us (30%)
  Pallas kernels  56.6 us (9%)
  local copies, waits for them, and re-layouts  44.5 us (7%)
  matrix products  22.8 us (3%)
  other arithmetic  21.7 us (3%)
  starting transfers between devices  16.1 us (2%)
  between operations  15 us (2%)
    all_to_all x1, blocking collectives, local(): lax.all_to_all(picked_rows.reshape(expert_count, capacity, normed_rows.sh...  101 us
    all_gather x4, waiting for transfers between devices, local(): lax.all_gather(prefix_cache[chunk * piece:(chunk + 1) * piece], 'req', ax...  99.4 us
    all_to_all x1, waiting for transfers between devices, local(): lax.all_to_all(send_results, 'req', split_axis=0, concat_axis=0, tiled=True)  98.6 us
    unnamed x8, waiting for transfers between devices  75 us
    pallas_call x4, Pallas kernels, prefix_attention(): pl.pallas_call(kernel, out_shape=(jax.ShapeDtypeStruct((rows, 1), jnp.flo...  56.6 us
    all_gather x1, blocking collectives, local(): full_rows = lax.all_gather(hidden_states.T, 'tp', axis=0, tiled=True).T  32.6 us
    all_gather x1, blocking collectives, local(): resid_rows = lax.all_gather(resid.T, 'tp', axis=0, tiled=True).T  29.6 us
    all_gather x1, blocking collectives, local(): router_full = lax.all_gather(router_weight, 'tp', axis=0, tiled=True)  29.3 us
  transfers between devices with their start and end apart: 7, of which 6 were waited for; matrix products, arithmetic and copies ran while one was open for 5% of the time, Pallas kernels for 7%

profile of v2, /device:TPU:8, one launch (start us, length us, event | category | flops | bytes accessed | tf_op | source)
XLA Modules:
  0.0 642.4 jit_solution(11737783514947524660)
XLA Ops:
  11.2 32.6 %all_gather.21 = bf16[2880,128]{1,0:T(8,128)(2,1)} all-gather(bf16[360,128]{1,0:T(8,128)(2,1)} %bitcast.95), channel_id=1, replica_groups=mesh['req'=32,'tp'=8] {'tp'}, dimensions={0}, use_global_device_ids=true | all-gather | bytes 829440 | tf_op jit(solution)/shard_map/all_gather | solution.py:147
  43.8 29.3 %all-gather = bf16[8,360,32]{1,2,0:T(8,128)(2,1)S(1)} all-gather(bf16[1,360,32]{1,2,0:T(8,128)(2,1)} %bitcast.103), channel_id=1, replica_groups=mesh['req'=32,'tp'=8] {'tp'}, dimensions={0}, use_global_device_ids=true | all-gather | bytes 207360 | tf_op jit(solution)/shard_map/all_gather | solution.py:148
  82.5 4.7 copy.89
  89.8 14.1 %shard_map.149 = (f32[1024,1]{1,0:T(8,128)}, f32[1024,1]{1,0:T(8,128)}, f32[1024,128]{1,0:T(8,128)}) custom-call(s32[1]{0:T(128)} %dynamic_slice.7.group_ref, bf16[1024,128]{1,0:T(8,128)(2,1)} %concatenate.36.q_ref, bf16[8192,128]{1,0:T(8,128)(2,1)} %all-gather.12.cloned.1.call-done.kv_ref, f32[1024,1]{1,0:T(8,128)} %copy-done.2, ...), custom_call_target="tpu_custom_call" | custom-call | flops 2147483648 | bytes 2359296 | tf_op jit(solution)/shard_map/pallas_call | solution.py:85
  103.9 18.5 %all-gather.10.cloned.1.call-done.kv_ref = bf16[8192,128]{1,0:T(8,128)(2,1)} async-done(((bf16[256,128]{1,0:T(8,128)(2,1)}), bf16[8192,128]{1,0:T(8,128)(2,1)}) %all-gather.10.cloned.1.call-update) | async-done | bytes 2097168 | tf_op jit(solution)/shard_map/all_gather | solution.py:192
  122.4 14.1 %shard_map.150 = (f32[1024,1]{1,0:T(8,128)}, f32[1024,1]{1,0:T(8,128)}, f32[1024,128]{1,0:T(8,128)}) custom-call(s32[1]{0:T(128)} %dynamic_slice.7.group_ref, bf16[1024,128]{1,0:T(8,128)(2,1)} %concatenate.36.q_ref, bf16[8192,128]{1,0:T(8,128)(2,1)} %all-gather.10.cloned.1.call-done.kv_ref, f32[1024,1]{1,0:T(8,128)} %get-tuple-element.16.m0_ref, ...), custom_call_target="tpu_custom_call" | custom-call | flops 2147483648 | bytes 2359296 | tf_op jit(solution)/shard_map/pallas_call | solution.py:85
  136.5 40.8 %all-gather.8.cloned.1.call-done.kv_ref = bf16[8192,128]{1,0:T(8,128)(2,1)} async-done(((bf16[256,128]{1,0:T(8,128)(2,1)}), bf16[8192,128]{1,0:T(8,128)(2,1)}) %all-gather.8.cloned.1.call-update) | async-done | bytes 2097168 | tf_op jit(solution)/shard_map/all_gather | solution.py:192
  177.3 14.1 %shard_map.151 = (f32[1024,1]{1,0:T(8,128)}, f32[1024,1]{1,0:T(8,128)}, f32[1024,128]{1,0:T(8,128)}) custom-call(s32[1]{0:T(128)} %dynamic_slice.7.group_ref, bf16[1024,128]{1,0:T(8,128)(2,1)} %concatenate.36.q_ref, bf16[8192,128]{1,0:T(8,128)(2,1)} %all-gather.8.cloned.1.call-done.kv_ref, f32[1024,1]{1,0:T(8,128)} %get-tuple-element.19.m0_ref, ...), custom_call_target="tpu_custom_call" | custom-call | flops 2147483648 | bytes 2359296 | tf_op jit(solution)/shard_map/pallas_call | solution.py:85
  191.4 40.1 %all-gather.6.cloned.1.call-done.kv_ref = bf16[8192,128]{1,0:T(8,128)(2,1)} async-done(((bf16[256,128]{1,0:T(8,128)(2,1)}), bf16[8192,128]{1,0:T(8,128)(2,1)}) %all-gather.6.cloned.1.call-update) | async-done | bytes 2097168 | tf_op jit(solution)/shard_map/all_gather | solution.py:192
  231.5 14.3 %shard_map.152 = (f32[1024,1]{1,0:T(8,128)}, f32[1024,1]{1,0:T(8,128)}, f32[1024,128]{1,0:T(8,128)}) custom-call(s32[1]{0:T(128)} %dynamic_slice.7.group_ref, bf16[1024,128]{1,0:T(8,128)(2,1)} %concatenate.36.q_ref, bf16[8192,128]{1,0:T(8,128)(2,1)} %all-gather.6.cloned.1.call-done.kv_ref, f32[1024,1]{1,0:T(8,128)} %get-tuple-element.22.m0_ref, ...), custom_call_target="tpu_custom_call" | custom-call | flops 2147483648 | bytes 2359296 | tf_op jit(solution)/shard_map/pallas_call | solution.py:85
  248.4 5.4 convolution_bitcast_fusion
  261.0 34.3 %reduce-scatter.9.cloned.1.call-done = f32[128,360]{0,1:T(8,128)} async-done(((f32[128,2880]{0,1:T(8,128)}), f32[128,360]{0,1:T(8,128)}) %reduce-scatter.9.cloned.1.call-update) | async-done | bytes 184336
  296.3 29.6 %all_gather.27 = bf16[2880,128]{1,0:T(8,128)(2,1)S(1)} all-gather(bf16[360,128]{1,0:T(8,128)(2,1)S(1)} %fusion.30), channel_id=1, replica_groups=mesh['req'=32,'tp'=8] {'tp'}, dimensions={0}, use_global_device_ids=true | all-gather | bytes 829440 | tf_op jit(solution)/shard_map/all_gather | solution.py:229
  326.7 4.9 gather_fusion
  334.3 101.2 %all_to_all.10 = bf16[32,24,2880]{2,1,0:T(8,128)(2,1)S(1)} all-to-all(bf16[32,24,2880]{2,1,0:T(8,128)(2,1)S(1)} %broadcast_select_fusion), channel_id=1, replica_groups=mesh['req'=32,'tp'=8] {'req'}, dimensions={0} | all-to-all | bytes 8847360 | tf_op jit(solution)/shard_map/all_to_all | solution.py:232
  435.5 6.2 convolution_bitcast_fusion.1
  441.7 4.6 convolution_convert_fusion
  446.3 15.8 %all-to-all-start.1 = ((bf16[32,24,2880]{2,1,0:T(8,128)(2,1)}), bf16[32,24,2880]{2,1,0:T(8,128)(2,1)}, u32[]{:S(2)}, u32[]{:S(2)}) async-start(bf16[32,24,2880]{2,1,0:T(8,128)(2,1)} %convolution_convert_fusion), calls=%async_computation.1 | async-start | bytes 9043968 | tf_op jit(solution)/shard_map/all_to_all | solution.py:253
  462.9 4.0 gather_fusion.2
  467.2 98.6 %all-to-all-done.1 = bf16[32,24,2880]{2,1,0:T(8,128)(2,1)} async-done(((bf16[32,24,2880]{2,1,0:T(8,128)(2,1)}), bf16[32,24,2880]{2,1,0:T(8,128)(2,1)}, u32[]{:S(2)}, u32[]{:S(2)}) %all-to-all-start.1) | async-done | bytes 4423712 | tf_op jit(solution)/shard_map/all_to_all | solution.py:253
  565.8 9.7 %gather_fusion.1 = bf16[512,2880]{1,0:T(8,128)(2,1)} fusion(bf16[768,2880]{1,0:T(8,128)(2,1)} %bitcast.37, s32[1024]{0:T(1024)S(1)} %pad_clamp_fusion), kind=kCustom, calls=%fused_computation.1 | custom fusion | bytes 5900288 | tf_op jit(solution)/shard_map/gather | solution.py:258
  575.5 6.5 %reshape.378 = f32[128,4,2880]{2,1,0:T(4,128)} reshape(bf16[512,2880]{1,0:T(8,128)(2,1)} %gather_fusion.1) | data formatting | bytes 8847360 | tf_op jit(solution)/shard_map/convert_element_type | solution.py:260
  582.1 8.3 %multiply_reduce_fusion = f32[128,2880]{1,0:T(8,128)} fusion(f32[128,4,2880]{2,1,0:T(4,128)} %reshape.378, f32[128,4]{1,0:T(8,128)S(1)} %copy.98), kind=kLoop, calls=%fused_computation.5 | loop fusion | flops 2580480 | bytes 7374848 | tf_op jit(solution)/shard_map/reduce_sum | solution.py:259
  594.7 38.8 %reduce-scatter.11.cloned.1.call-done = f32[128,360]{0,1:T(8,128)} async-done(((f32[128,2880]{0,1:T(8,128)}), f32[128,360]{0,1:T(8,128)}) %reduce-scatter.11.cloned.1.call-update) | async-done | bytes 184336
  (108 shorter events, 37.0 us)
Async XLA Ops:
  7.2 67.8 %copy-start = (bf16[2880,512]{1,0:T(8,128)(2,1)S(1)}, bf16[2880,512]{1,0:T(8,128)(2,1)}, u32[]{:S(2)}) copy-start(bf16[2880,512]{1,0:T(8,128)(2,1)} %param.16) | copy-start | bytes 8847364
  7.2 67.8 %copy-start.9 = (f32[2880]{0:T(1024)S(1)}, f32[2880]{0:T(1024)}, u32[]{:S(2)}) copy-start(f32[2880]{0:T(1024)} %param.15) | copy-start | bytes 34564
  7.2 82.6 %all-gather.12.cloned.1.call-start = ((), (), s32[]{:S(2)}) async-start(), calls=%async_computation.7 | async-start | bytes 2162688 | tf_op jit(solution)/shard_map/all_gather | solution.py:192
  9.0 113.4 %all-gather.10.cloned.1.call-start = ((), (), s32[]{:S(2)}) async-start(), calls=%async_computation.6 | async-start | bytes 2162688 | tf_op jit(solution)/shard_map/all_gather | solution.py:192
  9.8 167.5 %all-gather.8.cloned.1.call-start = ((), (), s32[]{:S(2)}) async-start(), calls=%async_computation.5 | async-start | bytes 2162688 | tf_op jit(solution)/shard_map/all_gather | solution.py:192
  10.5 221.0 %all-gather.6.cloned.1.call-start = ((), (), s32[]{:S(2)}) async-start(), calls=%async_computation.4 | async-start | bytes 2162688 | tf_op jit(solution)/shard_map/all_gather | solution.py:192
  11.1 284.2 %reduce-scatter.9.cloned.1.call-start = ((), (), s32[]{:S(2)}) async-start(), calls=%async_computation.8 | async-start | bytes 1658880
  77.7 2.9 copy-start.7
  81.6 7.3 %copy-start.2 = (f32[1024,1]{1,0:T(8,128)}, f32[1024,1]{1,0:T(8,128)S(1)}, u32[]{:S(2)}) copy-start(f32[1024,1]{1,0:T(8,128)S(1)} %copy.88.m0_ref) | copy-start | bytes 12292
  82.5 4.7 copy-start.10
  248.4 5.4 copy-start.5
  253.8 41.5 %copy-start.4 = (bf16[128,360]{0,1:T(8,128)(2,1)S(1)}, bf16[128,360]{0,1:T(8,128)(2,1)}, u32[]{:S(2)}) copy-start(bf16[128,360]{0,1:T(8,128)(2,1)} %param.14) | copy-start | bytes 276484
  253.9 72.6 %copy-start.6 = (f32[2880]{0:T(1024)S(1)}, f32[2880]{0:T(1024)}, u32[]{:S(2)}) copy-start(f32[2880]{0:T(1024)} %param.21) | copy-start | bytes 34564
  435.5 6.2 copy-start.8
  446.3 119.5 %all-to-all-start.1 = ((bf16[32,24,2880]{2,1,0:T(8,128)(2,1)}), bf16[32,24,2880]{2,1,0:T(8,128)(2,1)}, u32[]{:S(2)}, u32[]{:S(2)}) async-start(bf16[32,24,2880]{2,1,0:T(8,128)(2,1)} %convolution_convert_fusion), calls=%async_computation.1 | async-start | bytes 9043968 | tf_op jit(solution)/shard_map/all_to_all | solution.py:253
  462.1 171.3 %reduce-scatter.11.cloned.1.call-start = ((), (), s32[]{:S(2)}) async-start(), calls=%async_computation.9 | async-start | bytes 1658880
  582.1 53.0 %copy-start.1 = (bf16[2880,512]{1,0:T(8,128)(2,1)S(1)}, bf16[2880,512]{1,0:T(8,128)(2,1)}, u32[]{:S(2)}) copy-start(bf16[2880,512]{1,0:T(8,128)(2,1)} %param.16) | copy-start | bytes 8847364
  590.4 3.0 copy-start.11
  590.4 43.1 %copy-start.3 = (f32[128,360]{0,1:T(8,128)S(1)}, f32[128,360]{0,1:T(8,128)}, u32[]{:S(2)}) copy-start(f32[128,360]{0,1:T(8,128)} %reduce-scatter.9.cloned.1.call-done) | copy-start | bytes 552964
Sparse Core Ops, SparseCore 0:
  11.2 57.1 all-gather.11
  70.9 51.4 all-gather.9
  125.6 51.7 all-gather.7
  179.7 51.7 all-gather.5
  254.0 41.3 reduce-scatter.8
  593.5 39.8 reduce-scatter.10

commit v3 on v1

--- a/solution.py
+++ b/solution.py
@@ -136,8 +136,11 @@
     cache_rows = prefix_cache.shape[0]
     prefix_len = cache_rows * req_count // 2
     score_scale = head_size ** (-0.5)
-    router_full = lax.all_gather(router_weight, "tp", axis=0, tiled=True)
-    full_rows = lax.all_gather(hidden_states, "tp", axis=1, tiled=True)
+    col_count = hidden_states.shape[1]
+    packed = jnp.concatenate([hidden_states.T, router_weight], axis=1)
+    gathered = lax.all_gather(packed, "tp", axis=0, tiled=True)
+    full_rows = gathered[:, :token_count].T
+    router_full = gathered[:, token_count:]
     normed_attn = rms_rows(full_rows, attn_gain)
     positions = (prefix_len + jnp.arange(token_count, dtype=jnp.int32)).astype(jnp.float32)
     queries = jnp.dot(normed_attn, query_weight, preferred_element_type=jnp.float32)
@@ -188,11 +191,10 @@
         out_weight.reshape(local_heads, head_size, model_width),
         preferred_element_type=jnp.float32,
     )
-    attn_sum = lax.psum_scatter(attn_part, "tp", scatter_dimension=1, tiled=True)
-    col_count = attn_sum.shape[1]
+    attn_full = lax.psum(attn_part, "tp")
+    attn_sum = lax.dynamic_slice_in_dim(attn_full, tp_index * col_count, col_count, 1)
     live = (jnp.arange(token_count, dtype=jnp.int32) < suffix_lengths[req_index])[:, None]
     attn_out = jnp.where(live, attn_sum, 0.0).astype(jnp.bfloat16)
-    resid = (hidden_states.astype(jnp.float32) + attn_sum).astype(jnp.bfloat16)
     expert_count = router_weight.shape[1]
     top_count = route_ids.shape[1]
     capacity = token_count * top_count * 3 // (2 * expert_count)
@@ -209,7 +211,7 @@
     exp_local = gate_up_weight.shape[0]
     ff_local = gate_up_weight.shape[3]
     joined_weight = gate_up_weight.reshape(exp_local, model_width, 2 * ff_local)
-    resid_rows = lax.all_gather(resid, "tp", axis=1, tiled=True)
+    resid_rows = (full_rows.astype(jnp.float32) + attn_full).astype(jnp.bfloat16)
     normed_rows = rms_rows(resid_rows, ffn_gain)
     picked_rows = jnp.where(filled[:, None], normed_rows[source_of], jnp.zeros((), jnp.bfloat16))
     arrived = lax.all_to_all(

time: 560 us -> 550 us (0.982)
  blocking collectives: 281 us -> 126 us
  waiting for transfers between devices: 114 us -> 240 us
  local copies, waits for them, and re-layouts: 43.7 us -> 52.1 us
  starting transfers between devices: 21.1 us -> 26.9 us
    all_gather x3 -> x1, blocking collectives: 185 us -> 35.2 us  [local(): gathered = lax.all_gather(packed, 'tp', axis=0, tiled=True)]
    all_to_all x1, waiting for transfers between devices: 0.01 us -> 98.7 us  [local(): lax.all_to_all(send_results, 'req', split_axis=0, concat_axis=0, tiled=True)]
    psum x0 -> x1, waiting for transfers between devices: none -> 74.4 us  [local(): attn_full = lax.psum(attn_part, 'tp')]
    unnamed x5 -> x4, waiting for transfers between devices: 77.2 us -> 39.5 us
    all_gather x1, waiting for transfers between devices: 36.5 us -> 27.4 us  [local(): shard_rows = lax.all_gather(prefix_cache, 'req', axis=0, tiled=True)]
  transfers between devices with their start and end apart: 4 -> 4, of which waited for: 3 -> 4; matrix products, arithmetic and copies ran while one was open for 5% -> 7% of each run, Pallas kernels for 0% -> 0%
where the time goes in v3:
time: 550 us; the launch traced here: 549 us
  waiting for transfers between devices  240 us (44%)
  blocking collectives  126 us (23%)
  local copies, waits for them, and re-layouts  52.1 us (9%)
  Pallas kernels  45.3 us (8%)
  starting transfers between devices  26.9 us (5%)
  matrix products  22.6 us (4%)
  other arithmetic  21.8 us (4%)
  between operations  14.1 us (3%)
    all_to_all x1, waiting for transfers between devices, local(): lax.all_to_all(send_results, 'req', split_axis=0, concat_axis=0, tiled=True)  98.7 us
    all_to_all x1, blocking collectives, local(): lax.all_to_all(picked_rows.reshape(expert_count, capacity, normed_rows.sh...  91 us
    psum x1, waiting for transfers between devices, local(): attn_full = lax.psum(attn_part, 'tp')  74.4 us
    pallas_call x1, Pallas kernels, prefix_attention(): pl.pallas_call(kernel, out_shape=jax.ShapeDtypeStruct((rows, width), jnp....  45.3 us
    unnamed x4, waiting for transfers between devices  39.5 us
    all_gather x1, blocking collectives, local(): gathered = lax.all_gather(packed, 'tp', axis=0, tiled=True)  35.2 us
    all_gather x1, waiting for transfers between devices, local(): shard_rows = lax.all_gather(prefix_cache, 'req', axis=0, tiled=True)  27.4 us
    all_to_all x1, starting transfers between devices, local(): lax.all_to_all(send_results, 'req', split_axis=0, concat_axis=0, tiled=True)  26.6 us
  transfers between devices with their start and end apart: 4, of which 4 were waited for; matrix products, arithmetic and copies ran while one was open for 7% of the time, Pallas kernels for 0%

profile of v3, /device:TPU:8, one launch (start us, length us, event | category | flops | bytes accessed | tf_op | source)
XLA Modules:
  0.0 548.8 jit_solution(16377500350535238439)
XLA Ops:
  11.6 35.2 %all-gather = bf16[8,360,160]{1,2,0:T(8,128)(2,1)} all-gather(bf16[1,360,160]{1,2,0:T(8,128)(2,1)S(1)} %maximum_bitcast_fusion.1), channel_id=1, replica_groups=mesh['req'=32,'tp'=8] {'tp'}, dimensions={0}, use_global_device_ids=true | all-gather | bytes 1036800 | tf_op jit(solution)/shard_map/all_gather | solution.py:141
  46.8 2.6 copy.64
  51.0 2.7 fusion.27
  55.2 2.0 fusion.25
  59.2 4.7 copy.71
  66.4 27.4 %all-gather.3.cloned.1.call-done.kv_ref = bf16[32768,128]{1,0:T(8,128)(2,1)} async-done(((bf16[1024,128]{1,0:T(8,128)(2,1)}), bf16[32768,128]{1,0:T(8,128)(2,1)}) %all-gather.3.cloned.1.call-update) | async-done | bytes 8388624 | tf_op jit(solution)/shard_map/all_gather | solution.py:182
  93.7 45.3 %shard_map.149 = bf16[1024,128]{1,0:T(8,128)(2,1)} custom-call(s32[1]{0:T(128)} %dynamic_slice.10.group_ref, bf16[1024,128]{1,0:T(8,128)(2,1)} %concatenate.40.q_ref, bf16[32768,128]{1,0:T(8,128)(2,1)} %all-gather.3.cloned.1.call-done.kv_ref, f32[1024,1]{1,0:T(8,128)} %copy-done.5, f32[1024,1]{1,0:T(8,128)} %exponential_add_fusion.l0_ref, ...), custom_call_target="tpu_custom_call" | custom-call | flops 8589934592 | bytes 5242880 | tf_op jit(solution)/shard_map/pallas_call | solution.py:81
  140.1 5.4 convolution_bitcast_fusion
  148.3 2.6 scatter_custom_fusion.1
  151.0 2.4 scatter_custom_fusion
  153.5 74.4 %all-reduce.4.cloned.1.call-done = f32[128,2880]{0,1:T(8,128)} async-done(((f32[128,2880]{0,1:T(8,128)}), f32[128,2880]{0,1:T(8,128)}) %all-reduce.4.cloned.1.call-update) | async-done | bytes 1474576 | tf_op jit(solution)/shard_map/psum | solution.py:194
  232.6 4.9 gather_fusion
  237.5 2.8 broadcast_select_fusion
  240.3 91.0 %all_to_all.10 = bf16[32,24,2880]{2,1,0:T(8,128)(2,1)S(1)} all-to-all(bf16[32,24,2880]{2,1,0:T(8,128)(2,1)S(1)} %broadcast_select_fusion), channel_id=1, replica_groups=mesh['req'=32,'tp'=8] {'req'}, dimensions={0} | all-to-all | bytes 8847360 | tf_op jit(solution)/shard_map/all_to_all | solution.py:217
  331.3 6.2 %convolution_bitcast_fusion.1 = f32[32,1,24,720]{3,2,0,1:T(8,128)S(1)} fusion(bf16[32,24,2880]{2,1,0:T(8,128)(2,1)S(1)} %all_to_all.10, bf16[2880,720,1]{0,1,2:T(8,128)(2,1)} %bitcast.126), kind=kOutput, calls=%fused_computation.12 | convolution fusion | flops 3185049600 | bytes 10782720 | tf_op jit(solution)/shard_map/sepd,edf->sepf/dot_general | solution.py:226
  337.5 4.6 convolution_convert_fusion
  342.1 26.6 %all-to-all-start.1 = ((bf16[32,24,2880]{2,1,0:T(8,128)(2,1)}), bf16[32,24,2880]{2,1,0:T(8,128)(2,1)}, u32[]{:S(2)}, u32[]{:S(2)}) async-start(bf16[32,24,2880]{2,1,0:T(8,128)(2,1)} %convolution_convert_fusion), calls=%async_computation.1 | async-start | bytes 9043968 | tf_op jit(solution)/shard_map/all_to_all | solution.py:238
  369.6 3.7 gather_fusion.2
  373.7 98.7 %all-to-all-done.1 = bf16[32,24,2880]{2,1,0:T(8,128)(2,1)} async-done(((bf16[32,24,2880]{2,1,0:T(8,128)(2,1)}), bf16[32,24,2880]{2,1,0:T(8,128)(2,1)}, u32[]{:S(2)}, u32[]{:S(2)}) %all-to-all-start.1) | async-done | bytes 4423712 | tf_op jit(solution)/shard_map/all_to_all | solution.py:238
  472.3 9.7 %gather_fusion.1 = bf16[512,2880]{1,0:T(8,128)(2,1)} fusion(bf16[768,2880]{1,0:T(8,128)(2,1)} %bitcast.36, s32[1024]{0:T(1024)S(1)} %pad_clamp_fusion), kind=kCustom, calls=%fused_computation.1 | custom fusion | bytes 5900288 | tf_op jit(solution)/shard_map/gather | solution.py:243
  482.0 6.5 %reshape.378 = f32[128,4,2880]{2,1,0:T(4,128)} reshape(bf16[512,2880]{1,0:T(8,128)(2,1)} %gather_fusion.1) | data formatting | bytes 8847360 | tf_op jit(solution)/shard_map/convert_element_type | solution.py:245
  488.6 8.1 %multiply_reduce_fusion = f32[128,2880]{1,0:T(8,128)} fusion(f32[128,4,2880]{2,1,0:T(4,128)} %reshape.378, f32[128,4]{1,0:T(8,128)S(1)} %copy.80), kind=kLoop, calls=%fused_computation.5 | loop fusion | flops 2580480 | bytes 7374848 | tf_op jit(solution)/shard_map/reduce_sum | solution.py:244
  496.7 3.2 copy.81
  501.8 38.8 %reduce-scatter.5.cloned.1.call-done = f32[128,360]{0,1:T(8,128)} async-done(((f32[128,2880]{0,1:T(8,128)}), f32[128,360]{0,1:T(8,128)}) %reduce-scatter.5.cloned.1.call-update) | async-done | bytes 184336
  (96 shorter events, 25.4 us)
Async XLA Ops:
  7.2 43.9 %copy-start = (bf16[2880,512]{1,0:T(8,128)(2,1)S(1)}, bf16[2880,512]{1,0:T(8,128)(2,1)}, u32[]{:S(2)}) copy-start(bf16[2880,512]{1,0:T(8,128)(2,1)} %param.16) | copy-start | bytes 8847364
  7.2 86.6 %all-gather.3.cloned.1.call-start = ((), (), s32[]{:S(2)}) async-start(), calls=%async_computation.3 | async-start | bytes 8650752 | tf_op jit(solution)/shard_map/all_gather | solution.py:182
  7.9 220.0 %all-reduce.4.cloned.1.call-start = ((), (), s32[]{:S(2)}) async-start(), calls=%async_computation.4 | async-start | bytes 2949120 | tf_op jit(solution)/shard_map/psum | solution.py:194
  46.8 4.3 copy-start.11
  53.8 1.5 copy-start.2
  55.2 2.7 copy-start.9
  57.9 7.5 %copy-start.5 = (f32[1024,1]{1,0:T(8,128)}, f32[1024,1]{1,0:T(8,128)S(1)}, u32[]{:S(2)}) copy-start(f32[1024,1]{1,0:T(8,128)S(1)} %copy.70.m0_ref) | copy-start | bytes 12292
  59.2 4.7 copy-start.12
  63.8 1.6 copy-start.6
  145.5 0.7 copy-start.7
  146.2 83.7 %copy-start.8 = (f32[2880]{0:T(1024)S(1)}, f32[2880]{0:T(1024)}, u32[]{:S(2)}) copy-start(f32[2880]{0:T(1024)} %param.21) | copy-start | bytes 34564
  228.0 1.9 copy-start.4
  331.3 6.2 %copy-start.10 = (bf16[1,360,2880]{2,1,0:T(8,128)(2,1)S(1)}, bf16[1,360,2880]{2,1,0:T(8,128)(2,1)}, u32[]{:S(2)}) copy-start(bf16[1,360,2880]{2,1,0:T(8,128)(2,1)} %param.24) | copy-start | bytes 6220804
  342.1 27.1 %copy-start.3 = (bf16[128,2880]{0,1:T(8,128)(2,1)S(1)}, bf16[128,2880]{0,1:T(8,128)(2,1)}, u32[]{:S(2)}) copy-start(bf16[128,2880]{0,1:T(8,128)(2,1)} %fusion.3) | copy-start | bytes 2211844
  342.1 130.3 %all-to-all-start.1 = ((bf16[32,24,2880]{2,1,0:T(8,128)(2,1)}), bf16[32,24,2880]{2,1,0:T(8,128)(2,1)}, u32[]{:S(2)}, u32[]{:S(2)}) async-start(bf16[32,24,2880]{2,1,0:T(8,128)(2,1)} %convolution_convert_fusion), calls=%async_computation.1 | async-start | bytes 9043968 | tf_op jit(solution)/shard_map/all_to_all | solution.py:238
  368.7 171.9 %reduce-scatter.5.cloned.1.call-start = ((), (), s32[]{:S(2)}) async-start(), calls=%async_computation.5 | async-start | bytes 1658880
  496.7 45.6 %copy-start.1 = (bf16[2880,512]{1,0:T(8,128)(2,1)S(1)}, bf16[2880,512]{1,0:T(8,128)(2,1)}, u32[]{:S(2)}) copy-start(bf16[2880,512]{1,0:T(8,128)(2,1)} %param.16) | copy-start | bytes 8847364
  499.9 0.7 copy-start.13
Sparse Core Ops, SparseCore 0:
  10.6 83.1 all-gather.2
  145.7 82.2 all-reduce.3
  500.1 40.4 reduce-scatter.4

commit v4 on v3

--- a/solution.py
+++ b/solution.py
@@ -213,7 +213,14 @@
     joined_weight = gate_up_weight.reshape(exp_local, model_width, 2 * ff_local)
     resid_rows = (full_rows.astype(jnp.float32) + attn_full).astype(jnp.bfloat16)
     normed_rows = rms_rows(resid_rows, ffn_gain)
-    picked_rows = jnp.where(filled[:, None], normed_rows[source_of], jnp.zeros((), jnp.bfloat16))
+    slot_hit = (
+        targets.reshape(token_count, top_count)[:, :, None]
+        == jnp.arange(expert_count * capacity, dtype=jnp.int32)[None, None, :]
+    )
+    token_slot = jnp.any(slot_hit, axis=1).astype(jnp.bfloat16)
+    picked_rows = lax.dot_general(
+        token_slot, normed_rows, (((0,), (0,)), ((), ())), preferred_element_type=jnp.float32
+    ).astype(jnp.bfloat16)
     arrived = lax.all_to_all(
         picked_rows.reshape(expert_count, capacity, normed_rows.shape[1]),
         "req",
@@ -240,11 +247,12 @@
     chosen = jnp.take_along_axis(logits, route_ids, axis=1)
     raised = jnp.exp(chosen)
     gates = raised / jnp.sum(raised, axis=1, keepdims=True)
-    picked_back = returned.reshape(expert_count * capacity, model_width)[targets]
-    combined = jnp.sum(
-        picked_back.reshape(token_count, top_count, model_width).astype(jnp.float32)
-        * gates[:, :, None],
-        axis=1,
+    gate_slot = jnp.sum(jnp.where(slot_hit, gates[:, :, None], 0.0), axis=1)
+    combined = jnp.dot(
+        gate_slot,
+        returned.reshape(expert_count * capacity, model_width).astype(jnp.float32),
+        precision=lax.Precision.HIGHEST,
+        preferred_element_type=jnp.float32,
     )
     moe_sum = lax.psum_scatter(combined, "tp", scatter_dimension=1, tiled=True)
     moe_out = jnp.where(live, moe_sum, 0.0).astype(jnp.bfloat16)

time: 550 us -> 528 us (0.960)
  local copies, waits for them, and re-layouts: 52.1 us -> 29.7 us
  matrix products: 22.6 us -> 35.2 us
  other arithmetic: 21.8 us -> 11 us
    gather x2 -> x0, local copies, waits for them, and re-layouts: 14.6 us -> none  [the longest x1 9.7 us: local(): returned.reshape(expert_count * capacity, model_width)[targets]]
    dot_general x0 -> x2, matrix products: none -> 12 us  [the longest x1 8.24 us: local(): jnp.dot(gate_slot, returned.reshape(expert_count * capacity, model_width)...]
    reduce_sum x1, other arithmetic: 8.14 us -> 0.23 us  [local(): gate_slot = jnp.sum(jnp.where(slot_hit, gates[:, :, None], 0.0), axis=1)]
    psum x1, waiting for transfers between devices: 74.4 us -> 80.2 us  [local(): attn_full = lax.psum(attn_part, 'tp')]
where the time goes in v4:
time: 528 us; the launch traced here: 527 us
  waiting for transfers between devices  238 us (45%)
  blocking collectives  128 us (24%)
  Pallas kernels  45.2 us (9%)
  matrix products  35.2 us (7%)
  local copies, waits for them, and re-layouts  29.7 us (6%)
  starting transfers between devices  26.6 us (5%)
  between operations  14 us (3%)
  other arithmetic  11 us (2%)
    all_to_all x1, waiting for transfers between devices, local(): lax.all_to_all(send_results, 'req', split_axis=0, concat_axis=0, tiled=True)  96.8 us
    all_to_all x1, blocking collectives, local(): lax.all_to_all(picked_rows.reshape(expert_count, capacity, normed_rows.sh...  91.5 us
    psum x1, waiting for transfers between devices, local(): attn_full = lax.psum(attn_part, 'tp')  80.2 us
    pallas_call x1, Pallas kernels, prefix_attention(): pl.pallas_call(kernel, out_shape=jax.ShapeDtypeStruct((rows, width), jnp....  45.2 us
    unnamed x4, waiting for transfers between devices  38.4 us
    all_gather x1, blocking collectives, local(): gathered = lax.all_gather(packed, 'tp', axis=0, tiled=True)  36.2 us
    all_to_all x1, starting transfers between devices, local(): lax.all_to_all(send_results, 'req', split_axis=0, concat_axis=0, tiled=True)  26.5 us
    all_gather x1, waiting for transfers between devices, local(): shard_rows = lax.all_gather(prefix_cache, 'req', axis=0, tiled=True)  22.4 us
  transfers between devices with their start and end apart: 4, of which 4 were waited for; matrix products, arithmetic and copies ran while one was open for 7% of the time, Pallas kernels for 0%

profile of v4, /device:TPU:8, one launch (start us, length us, event | category | flops | bytes accessed | tf_op | source)
XLA Modules:
  0.0 527.1 jit_solution(16944720841401636628)
XLA Ops:
  9.8 36.2 %all-gather = bf16[8,360,160]{1,2,0:T(8,128)(2,1)} all-gather(bf16[1,360,160]{1,2,0:T(8,128)(2,1)S(1)} %maximum_bitcast_fusion.1), channel_id=1, replica_groups=mesh['req'=32,'tp'=8] {'tp'}, dimensions={0}, use_global_device_ids=true | all-gather | bytes 1036800 | tf_op jit(solution)/shard_map/all_gather | solution.py:141
  46.0 2.5 copy.89
  48.5 1.5 fusion.5
  50.2 2.7 fusion.30
  55.1 2.2 fusion.28
  61.5 4.7 copy.96
  68.6 1.9 exponential_add_fusion.l0_ref
  70.5 22.4 %all-gather.3.cloned.1.call-done.kv_ref = bf16[32768,128]{1,0:T(8,128)(2,1)} async-done(((bf16[1024,128]{1,0:T(8,128)(2,1)}), bf16[32768,128]{1,0:T(8,128)(2,1)}) %all-gather.3.cloned.1.call-update) | async-done | bytes 8388624 | tf_op jit(solution)/shard_map/all_gather | solution.py:182
  92.9 45.2 %shard_map.149 = bf16[1024,128]{1,0:T(8,128)(2,1)} custom-call(s32[1]{0:T(128)} %dynamic_slice.10.group_ref, bf16[1024,128]{1,0:T(8,128)(2,1)} %concatenate.40.q_ref, bf16[32768,128]{1,0:T(8,128)(2,1)} %all-gather.3.cloned.1.call-done.kv_ref, f32[1024,1]{1,0:T(8,128)} %copy.95.m0_ref, f32[1024,1]{1,0:T(8,128)} %exponential_add_fusion.l0_ref, ...), custom_call_target="tpu_custom_call" | custom-call | flops 8589934592 | bytes 5242880 | tf_op jit(solution)/shard_map/pallas_call | solution.py:81
  139.2 5.4 %convolution_bitcast_fusion = f32[128,2880]{0,1:T(8,128)} fusion(bf16[8,128,64]{2,1,0:T(8,128)(2,1)S(1)} %bitcast.108, bf16[8,64,2880]{2,1,0:T(8,128)(2,1)} %bitcast.104), kind=kOutput, calls=%fused_computation.3 | convolution fusion | flops 377487360 | bytes 4554752 | tf_op jit(solution)/shard_map/hqd,hdo->qo/dot_general | solution.py:188
  147.7 80.2 %all-reduce.4.cloned.1.call-done = f32[128,2880]{0,1:T(8,128)} async-done(((f32[128,2880]{0,1:T(8,128)}), f32[128,2880]{0,1:T(8,128)}) %all-reduce.4.cloned.1.call-update) | async-done | bytes 1474576 | tf_op jit(solution)/shard_map/psum | solution.py:194
  227.9 2.0 fusion.2
  230.7 3.8 convolution_convert_fusion.1
  234.5 6.5 %copy.104 = bf16[768,2880]{1,0:T(8,128)(2,1)} copy(bf16[768,2880]{0,1:T(8,128)(2,1)} %convolution_convert_fusion.1) | data formatting | bytes 8847360 | tf_op jit(solution)/shard_map/convert_element_type | solution.py:223
  241.0 91.5 %all_to_all.10 = bf16[32,24,2880]{2,1,0:T(8,128)(2,1)S(1)} all-to-all(bf16[32,24,2880]{2,1,0:T(8,128)(2,1)} %bitcast.98), channel_id=1, replica_groups=mesh['req'=32,'tp'=8] {'req'}, dimensions={0} | all-to-all | bytes 8847360 | tf_op jit(solution)/shard_map/all_to_all | solution.py:224
  332.5 3.8 convolution_bitcast_fusion.1
  336.4 4.5 convolution_convert_fusion
  340.9 26.5 %all-to-all-start.1 = ((bf16[32,24,2880]{2,1,0:T(8,128)(2,1)}), bf16[32,24,2880]{2,1,0:T(8,128)(2,1)}, u32[]{:S(2)}, u32[]{:S(2)}) async-start(bf16[32,24,2880]{2,1,0:T(8,128)(2,1)} %convolution_convert_fusion), calls=%async_computation.1 | async-start | bytes 9043968 | tf_op jit(solution)/shard_map/all_to_all | solution.py:245
  367.6 2.1 fusion.14
  369.8 4.0 gather_fusion
  374.2 96.8 %all-to-all-done.1 = bf16[32,24,2880]{2,1,0:T(8,128)(2,1)} async-done(((bf16[32,24,2880]{2,1,0:T(8,128)(2,1)}), bf16[32,24,2880]{2,1,0:T(8,128)(2,1)}, u32[]{:S(2)}, u32[]{:S(2)}) %all-to-all-start.1) | async-done | bytes 4423712 | tf_op jit(solution)/shard_map/all_to_all | solution.py:245
  471.0 8.2 %fusion.69 = f32[128,2880]{0,1:T(8,128)} fusion(f32[128,768]{1,0:T(8,128)S(1)} %select_reduce_fusion, bf16[768,2880]{1,0:T(8,128)(2,1)} %bitcast.35), kind=kOutput, calls=%fused_computation.110 | convolution fusion | flops 3397386240 | bytes 6291456 | tf_op jit(solution)/shard_map/dot_general | solution.py:251
  481.2 37.7 %reduce-scatter.5.cloned.1.call-done = f32[128,360]{0,1:T(8,128)} async-done(((f32[128,2880]{0,1:T(8,128)}), f32[128,360]{0,1:T(8,128)}) %reduce-scatter.5.cloned.1.call-update) | async-done | bytes 184336
  518.9 1.7 select_convert_fusion
  (86 shorter events, 19.1 us)
Async XLA Ops:
  7.2 43.0 %copy-start = (bf16[2880,512]{1,0:T(8,128)(2,1)S(1)}, bf16[2880,512]{1,0:T(8,128)(2,1)}, u32[]{:S(2)}) copy-start(bf16[2880,512]{1,0:T(8,128)(2,1)} %param.16) | copy-start | bytes 8847364
  7.2 85.7 %all-gather.3.cloned.1.call-start = ((), (), s32[]{:S(2)}) async-start(), calls=%async_computation.3 | async-start | bytes 8650752 | tf_op jit(solution)/shard_map/all_gather | solution.py:182
  7.9 220.0 %all-reduce.4.cloned.1.call-start = ((), (), s32[]{:S(2)}) async-start(), calls=%async_computation.4 | async-start | bytes 2949120 | tf_op jit(solution)/shard_map/psum | solution.py:194
  46.0 4.2 copy-start.10
  50.2 3.0 copy-start.8
  53.2 4.1 copy-start.2
  57.3 0.6 copy-start.6
  61.5 4.7 copy-start.11
  66.1 2.4 copy-start.3
  66.1 2.4 copy-start.4
  144.6 0.7 copy-start.5
  147.7 83.0 %copy-start.7 = (f32[2880]{0:T(1024)S(1)}, f32[2880]{0:T(1024)}, u32[]{:S(2)}) copy-start(f32[2880]{0:T(1024)} %param.21) | copy-start | bytes 34564
  229.8 0.9 copy-start.1
  234.5 98.0 %slice-start = ((s8[4239360]{0:T(1024)(128)(4,1)}), s8[45056]{0:T(1024)(128)(4,1)S(1)}, s32[]{:S(2)}) async-start(s8[4239360]{0:T(1024)(128)(4,1)} %bitcast.116), calls=%async_computation.6 | async-start | bytes 90112
  241.0 91.5 %slice-start.1 = ((s8[4239360]{0:T(1024)(128)(4,1)}), s8[4194304]{0:T(1024)(128)(4,1)S(1)}, s32[]{:S(2)}) async-start(s8[4239360]{0:T(1024)(128)(4,1)} %bitcast.116), calls=%async_computation.7 | async-start | bytes 8388608
  332.5 3.9 copy-start.9
  340.9 130.2 %all-to-all-start.1 = ((bf16[32,24,2880]{2,1,0:T(8,128)(2,1)}), bf16[32,24,2880]{2,1,0:T(8,128)(2,1)}, u32[]{:S(2)}, u32[]{:S(2)}) async-start(bf16[32,24,2880]{2,1,0:T(8,128)(2,1)} %convolution_convert_fusion), calls=%async_computation.1 | async-start | bytes 9043968 | tf_op jit(solution)/shard_map/all_to_all | solution.py:245
  367.4 151.5 %reduce-scatter.5.cloned.1.call-start = ((), (), s32[]{:S(2)}) async-start(), calls=%async_computation.5 | async-start | bytes 1658880
  479.3 0.7 copy-start.12
Sparse Core Ops, SparseCore 0:
  10.6 82.2 all-gather.2
  144.7 83.0 all-reduce.3
  479.4 39.4 reduce-scatter.4

commit v5 on v4

--- a/solution.py
+++ b/solution.py
@@ -191,8 +191,7 @@
         out_weight.reshape(local_heads, head_size, model_width),
         preferred_element_type=jnp.float32,
     )
-    attn_full = lax.psum(attn_part, "tp")
-    attn_sum = lax.dynamic_slice_in_dim(attn_full, tp_index * col_count, col_count, 1)
+    attn_sum = lax.psum_scatter(attn_part, "tp", scatter_dimension=1, tiled=True)
     live = (jnp.arange(token_count, dtype=jnp.int32) < suffix_lengths[req_index])[:, None]
     attn_out = jnp.where(live, attn_sum, 0.0).astype(jnp.bfloat16)
     expert_count = router_weight.shape[1]
@@ -211,7 +210,8 @@
     exp_local = gate_up_weight.shape[0]
     ff_local = gate_up_weight.shape[3]
     joined_weight = gate_up_weight.reshape(exp_local, model_width, 2 * ff_local)
-    resid_rows = (full_rows.astype(jnp.float32) + attn_full).astype(jnp.bfloat16)
+    resid = (hidden_states.astype(jnp.float32) + attn_sum).astype(jnp.bfloat16)
+    resid_rows = lax.all_gather(resid, "tp", axis=1, tiled=True)
     normed_rows = rms_rows(resid_rows, ffn_gain)
     slot_hit = (
         targets.reshape(token_count, top_count)[:, :, None]

time: 528 us -> 519 us (0.983)
  waiting for transfers between devices: 238 us -> 201 us
  blocking collectives: 128 us -> 160 us
    psum x1 -> x0, waiting for transfers between devices: 80.2 us -> none  [local(): attn_full = lax.psum(attn_part, 'tp')]
    unnamed x4 -> x5, waiting for transfers between devices: 38.4 us -> 82 us
    all_gather x0 -> x1, blocking collectives: none -> 29.7 us  [local(): resid_rows = lax.all_gather(resid, 'tp', axis=1, tiled=True)]
where the time goes in v5:
time: 519 us; the launch traced here: 518 us
  waiting for transfers between devices  201 us (39%)
  blocking collectives  160 us (31%)
  Pallas kernels  45.3 us (9%)
  matrix products  33.3 us (6%)
  local copies, waits for them, and re-layouts  30.7 us (6%)
  starting transfers between devices  22.4 us (4%)
  between operations  14 us (3%)
  other arithmetic  10.5 us (2%)
    all_to_all x1, waiting for transfers between devices, local(): lax.all_to_all(send_results, 'req', split_axis=0, concat_axis=0, tiled=True)  97.3 us
    all_to_all x1, blocking collectives, local(): lax.all_to_all(picked_rows.reshape(expert_count, capacity, normed_rows.sh...  95.8 us
    unnamed x5, waiting for transfers between devices  82 us
    pallas_call x1, Pallas kernels, prefix_attention(): pl.pallas_call(kernel, out_shape=jax.ShapeDtypeStruct((rows, width), jnp....  45.3 us
    all_gather x1, blocking collectives, local(): gathered = lax.all_gather(packed, 'tp', axis=0, tiled=True)  34.9 us
    all_gather x1, blocking collectives, local(): resid_rows = lax.all_gather(resid, 'tp', axis=1, tiled=True)  29.7 us
    all_to_all x1, starting transfers between devices, local(): lax.all_to_all(send_results, 'req', split_axis=0, concat_axis=0, tiled=True)  22 us
    all_gather x1, waiting for transfers between devices, local(): shard_rows = lax.all_gather(prefix_cache, 'req', axis=0, tiled=True)  22 us
  transfers between devices with their start and end apart: 4, of which 4 were waited for; matrix products, arithmetic and copies ran while one was open for 7% of the time, Pallas kernels for 0%

profile of v5, /device:TPU:8, one launch (start us, length us, event | category | flops | bytes accessed | tf_op | source)
XLA Modules:
  0.0 518.0 jit_solution(191498900962958838)
XLA Ops:
  9.8 34.9 %all-gather = bf16[8,360,160]{1,2,0:T(8,128)(2,1)S(1)} all-gather(bf16[1,360,160]{1,2,0:T(8,128)(2,1)S(1)} %maximum_bitcast_fusion.1), channel_id=1, replica_groups=mesh['req'=32,'tp'=8] {'tp'}, dimensions={0}, use_global_device_ids=true | all-gather | bytes 1036800 | tf_op jit(solution)/shard_map/all_gather | solution.py:141
  46.1 2.7 reshape.361
  50.4 2.4 fusion.29
  53.8 1.9 fusion.27
  59.7 1.7 concatenate.40.q_ref
  61.4 4.7 copy.116
  68.5 2.3 exponential_add_fusion.l0_ref
  70.8 22.0 %all-gather.3.cloned.1.call-done.kv_ref = bf16[32768,128]{1,0:T(8,128)(2,1)} async-done(((bf16[1024,128]{1,0:T(8,128)(2,1)}), bf16[32768,128]{1,0:T(8,128)(2,1)}) %all-gather.3.cloned.1.call-update) | async-done | bytes 8388624 | tf_op jit(solution)/shard_map/all_gather | solution.py:182
  92.8 45.3 %shard_map.149 = bf16[1024,128]{1,0:T(8,128)(2,1)} custom-call(s32[1]{0:T(128)} %dynamic_slice.7.group_ref, bf16[1024,128]{1,0:T(8,128)(2,1)} %concatenate.40.q_ref, bf16[32768,128]{1,0:T(8,128)(2,1)} %all-gather.3.cloned.1.call-done.kv_ref, f32[1024,1]{1,0:T(8,128)} %copy.115.m0_ref, f32[1024,1]{1,0:T(8,128)} %exponential_add_fusion.l0_ref, ...), custom_call_target="tpu_custom_call" | custom-call | flops 8589934592 | bytes 5242880 | tf_op jit(solution)/shard_map/pallas_call | solution.py:81
  139.1 5.4 %convolution_bitcast_fusion = f32[128,2880]{0,1:T(8,128)} fusion(bf16[8,128,64]{2,1,0:T(8,128)(2,1)S(1)} %bitcast.89, bf16[8,64,2880]{2,1,0:T(8,128)(2,1)} %bitcast.85), kind=kOutput, calls=%fused_computation.3 | convolution fusion | flops 377487360 | bytes 4554752 | tf_op jit(solution)/shard_map/hqd,hdo->qo/dot_general | solution.py:188
  147.0 39.6 %reduce-scatter.9.cloned.1.call-done = f32[128,360]{0,1:T(8,128)} async-done(((f32[128,2880]{0,1:T(8,128)}), f32[128,360]{0,1:T(8,128)}) %reduce-scatter.9.cloned.1.call-update) | async-done | bytes 184336
  187.5 29.7 %all_gather.11 = bf16[128,2880]{0,1:T(8,128)(2,1)S(1)} all-gather(bf16[128,360]{0,1:T(8,128)(2,1)S(1)} %add_convert_fusion), channel_id=1, replica_groups=mesh['req'=32,'tp'=8] {'tp'}, dimensions={1}, use_global_device_ids=true | all-gather | bytes 829440 | tf_op jit(solution)/shard_map/all_gather | solution.py:214
  218.2 3.8 convolution_convert_fusion.1
  222.0 6.5 %copy.124 = bf16[768,2880]{1,0:T(8,128)(2,1)} copy(bf16[768,2880]{0,1:T(8,128)(2,1)} %convolution_convert_fusion.1) | data formatting | bytes 8847360 | tf_op jit(solution)/shard_map/convert_element_type | solution.py:223
  228.5 95.8 %all_to_all.10 = bf16[32,24,2880]{2,1,0:T(8,128)(2,1)S(1)} all-to-all(bf16[32,24,2880]{2,1,0:T(8,128)(2,1)} %bitcast.84), channel_id=1, replica_groups=mesh['req'=32,'tp'=8] {'req'}, dimensions={0} | all-to-all | bytes 8847360 | tf_op jit(solution)/shard_map/all_to_all | solution.py:224
  324.3 3.8 convolution_bitcast_fusion.1
  328.2 4.5 convolution_convert_fusion
  332.7 22.0 %all-to-all-start.1 = ((bf16[32,24,2880]{2,1,0:T(8,128)(2,1)}), bf16[32,24,2880]{2,1,0:T(8,128)(2,1)}, u32[]{:S(2)}, u32[]{:S(2)}) async-start(bf16[32,24,2880]{2,1,0:T(8,128)(2,1)} %convolution_convert_fusion), calls=%async_computation.1 | async-start | bytes 9043968 | tf_op jit(solution)/shard_map/all_to_all | solution.py:245
  355.3 1.8 fusion.24
  357.1 3.7 gather_fusion
  361.3 97.3 %all-to-all-done.1 = bf16[32,24,2880]{2,1,0:T(8,128)(2,1)} async-done(((bf16[32,24,2880]{2,1,0:T(8,128)(2,1)}), bf16[32,24,2880]{2,1,0:T(8,128)(2,1)}, u32[]{:S(2)}, u32[]{:S(2)}) %all-to-all-start.1) | async-done | bytes 4423712 | tf_op jit(solution)/shard_map/all_to_all | solution.py:245
  458.6 8.3 %fusion.67 = f32[128,2880]{0,1:T(8,128)} fusion(f32[128,768]{1,0:T(8,128)S(1)} %select_reduce_fusion, bf16[768,2880]{1,0:T(8,128)(2,1)} %bitcast.33), kind=kOutput, calls=%fused_computation.109 | convolution fusion | flops 3397386240 | bytes 6291456 | tf_op jit(solution)/shard_map/dot_general | solution.py:251
  468.1 41.7 %reduce-scatter.11.cloned.1.call-done = f32[128,360]{0,1:T(8,128)} async-done(((f32[128,2880]{0,1:T(8,128)}), f32[128,360]{0,1:T(8,128)}) %reduce-scatter.11.cloned.1.call-update) | async-done | bytes 184336
  509.8 1.6 select_convert_fusion
  (89 shorter events, 20.4 us)
Async XLA Ops:
  7.2 43.2 %copy-start = (bf16[2880,512]{1,0:T(8,128)(2,1)S(1)}, bf16[2880,512]{1,0:T(8,128)(2,1)}, u32[]{:S(2)}) copy-start(bf16[2880,512]{1,0:T(8,128)(2,1)} %param.16) | copy-start | bytes 8847364
  7.2 85.6 %all-gather.3.cloned.1.call-start = ((), (), s32[]{:S(2)}) async-start(), calls=%async_computation.4 | async-start | bytes 8650752 | tf_op jit(solution)/shard_map/all_gather | solution.py:182
  7.9 178.7 %reduce-scatter.9.cloned.1.call-start = ((), (), s32[]{:S(2)}) async-start(), calls=%async_computation.5 | async-start | bytes 1658880
  46.1 4.2 copy-start.10
  53.8 2.1 copy-start.2
  53.8 2.5 copy-start.8
  55.6 0.6 copy-start.6
  61.4 4.7 copy-start.11
  139.1 5.4 %copy-start.5 = (s32[128,4]{0,1:T(4,128)S(1)}, s32[128,4]{0,1:T(4,128)}, u32[]{:S(2)}) copy-start(s32[128,4]{0,1:T(4,128)} %param.25) | copy-start | bytes 6148
  144.5 42.0 %copy-start.4 = (bf16[128,360]{0,1:T(8,128)(2,1)S(1)}, bf16[128,360]{0,1:T(8,128)(2,1)}, u32[]{:S(2)}) copy-start(bf16[128,360]{0,1:T(8,128)(2,1)} %param.14) | copy-start | bytes 276484
  144.6 73.6 %copy-start.7 = (f32[2880]{0:T(1024)S(1)}, f32[2880]{0:T(1024)}, u32[]{:S(2)}) copy-start(f32[2880]{0:T(1024)} %param.21) | copy-start | bytes 34564
  217.3 0.9 copy-start.1
  222.0 102.3 %slice-start = ((s8[4239360]{0:T(1024)(128)(4,1)}), s8[45056]{0:T(1024)(128)(4,1)S(1)}, s32[]{:S(2)}) async-start(s8[4239360]{0:T(1024)(128)(4,1)} %bitcast.97), calls=%async_computation.7 | async-start | bytes 90112
  228.5 95.8 %slice-start.1 = ((s8[4239360]{0:T(1024)(128)(4,1)}), s8[4194304]{0:T(1024)(128)(4,1)S(1)}, s32[]{:S(2)}) async-start(s8[4239360]{0:T(1024)(128)(4,1)} %bitcast.97), calls=%async_computation.8 | async-start | bytes 8388608
  324.3 3.9 copy-start.9
  332.7 125.8 %all-to-all-start.1 = ((bf16[32,24,2880]{2,1,0:T(8,128)(2,1)}), bf16[32,24,2880]{2,1,0:T(8,128)(2,1)}, u32[]{:S(2)}, u32[]{:S(2)}) async-start(bf16[32,24,2880]{2,1,0:T(8,128)(2,1)} %convolution_convert_fusion), calls=%async_computation.1 | async-start | bytes 9043968 | tf_op jit(solution)/shard_map/all_to_all | solution.py:245
  354.8 155.0 %reduce-scatter.11.cloned.1.call-start = ((), (), s32[]{:S(2)}) async-start(), calls=%async_computation.6 | async-start | bytes 1658880
  458.6 8.3 %copy-start.12 = (s32[32]{0:T(128)S(1)}, s32[32]{0:T(128)}, u32[]{:S(2)}) copy-start(s32[32]{0:T(128)} %param.27) | copy-start | bytes 388
  466.8 43.0 %copy-start.3 = (f32[128,360]{0,1:T(8,128)S(1)}, f32[128,360]{0,1:T(8,128)}, u32[]{:S(2)}) copy-start(f32[128,360]{0,1:T(8,128)} %reduce-scatter.9.cloned.1.call-done) | copy-start | bytes 552964
Sparse Core Ops, SparseCore 0:
  10.6 82.1 all-gather.2
  144.7 41.8 reduce-scatter.8
  467.0 42.7 reduce-scatter.10

commit v6 on v5

--- a/solution.py
+++ b/solution.py
@@ -74,7 +74,7 @@
 def prefix_attention(group, query, cache, peak, denominator, accum, *, prefix_len, scale):
     rows, width = query.shape
     block_q = min(rows, 1024)
-    block_k = 1024
+    block_k = 2048
     steps = prefix_len // block_k
     grid = (rows // block_q, steps)
     kernel = functools.partial(flash_kernel, scale=scale, steps=steps)

time: 519 us -> 510 us (0.983)
  Pallas kernels: 45.3 us -> 36.9 us
    pallas_call x1, Pallas kernels: 45.3 us -> 36.9 us  [prefix_attention(): pl.pallas_call(kernel, out_shape=jax.ShapeDtypeStruct((rows, width), jnp....]
where the time goes in v6:
time: 510 us; the launch traced here: 509 us
  waiting for transfers between devices  201 us (39%)
  blocking collectives  164 us (32%)
  Pallas kernels  36.9 us (7%)
  matrix products  33.3 us (7%)
  local copies, waits for them, and re-layouts  30.9 us (6%)
  starting transfers between devices  17.8 us (3%)
  between operations  14 us (3%)
  other arithmetic  10.6 us (2%)
    all_to_all x1, blocking collectives, local(): lax.all_to_all(picked_rows.reshape(expert_count, capacity, normed_rows.sh...  99.9 us
    all_to_all x1, waiting for transfers between devices, local(): lax.all_to_all(send_results, 'req', split_axis=0, concat_axis=0, tiled=True)  97.1 us
    unnamed x5, waiting for transfers between devices  82 us
    pallas_call x1, Pallas kernels, prefix_attention(): pl.pallas_call(kernel, out_shape=jax.ShapeDtypeStruct((rows, width), jnp....  36.9 us
    all_gather x1, blocking collectives, local(): gathered = lax.all_gather(packed, 'tp', axis=0, tiled=True)  34.9 us
    all_gather x1, blocking collectives, local(): resid_rows = lax.all_gather(resid, 'tp', axis=1, tiled=True)  29.5 us
    all_gather x1, waiting for transfers between devices, local(): shard_rows = lax.all_gather(prefix_cache, 'req', axis=0, tiled=True)  22 us
    all_to_all x1, starting transfers between devices, local(): lax.all_to_all(send_results, 'req', split_axis=0, concat_axis=0, tiled=True)  17.7 us
  transfers between devices with their start and end apart: 4, of which 4 were waited for; matrix products, arithmetic and copies ran while one was open for 7% of the time, Pallas kernels for 0%

profile of v6, /device:TPU:8, one launch (start us, length us, event | category | flops | bytes accessed | tf_op | source)
XLA Modules:
  0.0 509.1 jit_solution(10328157083671481951)
XLA Ops:
  9.8 34.9 %all-gather = bf16[8,360,160]{1,2,0:T(8,128)(2,1)S(1)} all-gather(bf16[1,360,160]{1,2,0:T(8,128)(2,1)S(1)} %maximum_bitcast_fusion.1), channel_id=1, replica_groups=mesh['req'=32,'tp'=8] {'tp'}, dimensions={0}, use_global_device_ids=true | all-gather | bytes 1036800 | tf_op jit(solution)/shard_map/all_gather | solution.py:141
  46.1 2.7 reshape.361
  50.4 2.4 fusion.29
  53.8 1.9 fusion.27
  59.7 1.7 concatenate.40.q_ref
  61.4 4.7 copy.116
  68.5 2.3 exponential_add_fusion.l0_ref
  70.8 22.0 %all-gather.3.cloned.1.call-done.kv_ref = bf16[32768,128]{1,0:T(8,128)(2,1)} async-done(((bf16[1024,128]{1,0:T(8,128)(2,1)}), bf16[32768,128]{1,0:T(8,128)(2,1)}) %all-gather.3.cloned.1.call-update) | async-done | bytes 8388624 | tf_op jit(solution)/shard_map/all_gather | solution.py:182
  92.8 36.9 %shard_map.149 = bf16[1024,128]{1,0:T(8,128)(2,1)} custom-call(s32[1]{0:T(128)} %dynamic_slice.7.group_ref, bf16[1024,128]{1,0:T(8,128)(2,1)} %concatenate.40.q_ref, bf16[32768,128]{1,0:T(8,128)(2,1)} %all-gather.3.cloned.1.call-done.kv_ref, f32[1024,1]{1,0:T(8,128)} %copy.115.m0_ref, f32[1024,1]{1,0:T(8,128)} %exponential_add_fusion.l0_ref, ...), custom_call_target="tpu_custom_call" | custom-call | flops 8589934592 | bytes 5242880 | tf_op jit(solution)/shard_map/pallas_call | solution.py:81
  130.7 5.4 %convolution_bitcast_fusion = f32[128,2880]{0,1:T(8,128)} fusion(bf16[8,128,64]{2,1,0:T(8,128)(2,1)S(1)} %bitcast.89, bf16[8,64,2880]{2,1,0:T(8,128)(2,1)} %bitcast.85), kind=kOutput, calls=%fused_computation.3 | convolution fusion | flops 377487360 | bytes 4554752 | tf_op jit(solution)/shard_map/hqd,hdo->qo/dot_general | solution.py:188
  138.7 39.5 %reduce-scatter.9.cloned.1.call-done = f32[128,360]{0,1:T(8,128)} async-done(((f32[128,2880]{0,1:T(8,128)}), f32[128,360]{0,1:T(8,128)}) %reduce-scatter.9.cloned.1.call-update) | async-done | bytes 184336
  179.2 29.5 %all_gather.11 = bf16[128,2880]{0,1:T(8,128)(2,1)S(1)} all-gather(bf16[128,360]{0,1:T(8,128)(2,1)S(1)} %add_convert_fusion), channel_id=1, replica_groups=mesh['req'=32,'tp'=8] {'tp'}, dimensions={1}, use_global_device_ids=true | all-gather | bytes 829440 | tf_op jit(solution)/shard_map/all_gather | solution.py:214
  209.6 3.8 convolution_convert_fusion.1
  213.4 6.5 %copy.124 = bf16[768,2880]{1,0:T(8,128)(2,1)} copy(bf16[768,2880]{0,1:T(8,128)(2,1)} %convolution_convert_fusion.1) | data formatting | bytes 8847360 | tf_op jit(solution)/shard_map/convert_element_type | solution.py:223
  219.9 99.9 %all_to_all.10 = bf16[32,24,2880]{2,1,0:T(8,128)(2,1)S(1)} all-to-all(bf16[32,24,2880]{2,1,0:T(8,128)(2,1)} %bitcast.84), channel_id=1, replica_groups=mesh['req'=32,'tp'=8] {'req'}, dimensions={0} | all-to-all | bytes 8847360 | tf_op jit(solution)/shard_map/all_to_all | solution.py:224
  319.8 3.8 convolution_bitcast_fusion.1
  323.7 4.5 convolution_convert_fusion
  328.2 17.7 %all-to-all-start.1 = ((bf16[32,24,2880]{2,1,0:T(8,128)(2,1)}), bf16[32,24,2880]{2,1,0:T(8,128)(2,1)}, u32[]{:S(2)}, u32[]{:S(2)}) async-start(bf16[32,24,2880]{2,1,0:T(8,128)(2,1)} %convolution_convert_fusion), calls=%async_computation.1 | async-start | bytes 9043968 | tf_op jit(solution)/shard_map/all_to_all | solution.py:245
  346.2 1.8 fusion.24
  348.0 4.0 gather_fusion
  352.4 97.1 %all-to-all-done.1 = bf16[32,24,2880]{2,1,0:T(8,128)(2,1)} async-done(((bf16[32,24,2880]{2,1,0:T(8,128)(2,1)}), bf16[32,24,2880]{2,1,0:T(8,128)(2,1)}, u32[]{:S(2)}, u32[]{:S(2)}) %all-to-all-start.1) | async-done | bytes 4423712 | tf_op jit(solution)/shard_map/all_to_all | solution.py:245
  449.6 8.3 %fusion.67 = f32[128,2880]{0,1:T(8,128)} fusion(f32[128,768]{1,0:T(8,128)S(1)} %select_reduce_fusion, bf16[768,2880]{1,0:T(8,128)(2,1)} %bitcast.33), kind=kOutput, calls=%fused_computation.109 | convolution fusion | flops 3397386240 | bytes 6291456 | tf_op jit(solution)/shard_map/dot_general | solution.py:251
  459.1 41.8 %reduce-scatter.11.cloned.1.call-done = f32[128,360]{0,1:T(8,128)} async-done(((f32[128,2880]{0,1:T(8,128)}), f32[128,360]{0,1:T(8,128)}) %reduce-scatter.11.cloned.1.call-update) | async-done | bytes 184336
  500.9 1.6 select_convert_fusion
  (89 shorter events, 20.3 us)
Async XLA Ops:
  7.2 43.2 %copy-start = (bf16[2880,512]{1,0:T(8,128)(2,1)S(1)}, bf16[2880,512]{1,0:T(8,128)(2,1)}, u32[]{:S(2)}) copy-start(bf16[2880,512]{1,0:T(8,128)(2,1)} %param.16) | copy-start | bytes 8847364
  7.2 85.6 %all-gather.3.cloned.1.call-start = ((), (), s32[]{:S(2)}) async-start(), calls=%async_computation.4 | async-start | bytes 8650752 | tf_op jit(solution)/shard_map/all_gather | solution.py:182
  7.9 170.3 %reduce-scatter.9.cloned.1.call-start = ((), (), s32[]{:S(2)}) async-start(), calls=%async_computation.5 | async-start | bytes 1658880
  46.1 4.2 copy-start.10
  53.8 2.1 copy-start.2
  53.8 2.5 copy-start.8
  55.6 0.6 copy-start.6
  61.4 4.7 copy-start.11
  130.7 5.4 %copy-start.5 = (s32[128,4]{0,1:T(4,128)S(1)}, s32[128,4]{0,1:T(4,128)}, u32[]{:S(2)}) copy-start(s32[128,4]{0,1:T(4,128)} %param.25) | copy-start | bytes 6148
  136.1 42.1 %copy-start.4 = (bf16[128,360]{0,1:T(8,128)(2,1)S(1)}, bf16[128,360]{0,1:T(8,128)(2,1)}, u32[]{:S(2)}) copy-start(bf16[128,360]{0,1:T(8,128)(2,1)} %param.14) | copy-start | bytes 276484
  136.2 73.4 %copy-start.7 = (f32[2880]{0:T(1024)S(1)}, f32[2880]{0:T(1024)}, u32[]{:S(2)}) copy-start(f32[2880]{0:T(1024)} %param.21) | copy-start | bytes 34564
  208.7 0.9 copy-start.1
  213.4 106.4 %slice-start = ((s8[4239360]{0:T(1024)(128)(4,1)}), s8[45056]{0:T(1024)(128)(4,1)S(1)}, s32[]{:S(2)}) async-start(s8[4239360]{0:T(1024)(128)(4,1)} %bitcast.97), calls=%async_computation.7 | async-start | bytes 90112
  219.9 99.9 %slice-start.1 = ((s8[4239360]{0:T(1024)(128)(4,1)}), s8[4194304]{0:T(1024)(128)(4,1)S(1)}, s32[]{:S(2)}) async-start(s8[4239360]{0:T(1024)(128)(4,1)} %bitcast.97), calls=%async_computation.8 | async-start | bytes 8388608
  319.8 3.9 copy-start.9
  328.2 121.3 %all-to-all-start.1 = ((bf16[32,24,2880]{2,1,0:T(8,128)(2,1)}), bf16[32,24,2880]{2,1,0:T(8,128)(2,1)}, u32[]{:S(2)}, u32[]{:S(2)}) async-start(bf16[32,24,2880]{2,1,0:T(8,128)(2,1)} %convolution_convert_fusion), calls=%async_computation.1 | async-start | bytes 9043968 | tf_op jit(solution)/shard_map/all_to_all | solution.py:245
  345.9 155.0 %reduce-scatter.11.cloned.1.call-start = ((), (), s32[]{:S(2)}) async-start(), calls=%async_computation.6 | async-start | bytes 1658880
  449.6 8.3 %copy-start.12 = (s32[32]{0:T(128)S(1)}, s32[32]{0:T(128)}, u32[]{:S(2)}) copy-start(s32[32]{0:T(128)} %param.27) | copy-start | bytes 388
  457.8 43.1 %copy-start.3 = (f32[128,360]{0,1:T(8,128)S(1)}, f32[128,360]{0,1:T(8,128)}, u32[]{:S(2)}) copy-start(f32[128,360]{0,1:T(8,128)} %reduce-scatter.9.cloned.1.call-done) | copy-start | bytes 552964
Sparse Core Ops, SparseCore 0:
  10.6 82.1 all-gather.2
  136.3 41.8 reduce-scatter.8
  458.0 42.9 reduce-scatter.10

commit v7 on v6

--- a/solution.py
+++ b/solution.py
@@ -241,20 +241,33 @@
     results = jnp.einsum(
         "sepf,efd->sepd", active, down_weight, preferred_element_type=jnp.float32
     ).astype(jnp.bfloat16)
-    send_results = results.reshape(arrived.shape[0], item_count, model_width)
-    returned = lax.all_to_all(send_results, "req", split_axis=0, concat_axis=0, tiled=True)
+    tp_count = lax.axis_size("tp")
+    feat_part = model_width // tp_count
+    send_results = (
+        results.reshape(req_count, item_count, tp_count, feat_part)
+        .transpose(0, 2, 1, 3)
+        .reshape(req_count * tp_count, item_count, feat_part)
+    )
+    returned = lax.all_to_all(
+        send_results, ("req", "tp"), split_axis=0, concat_axis=0, tiled=True
+    )
+    expert_parts = jnp.sum(
+        returned.reshape(req_count * exp_local, tp_count, item_count, feat_part).astype(
+            jnp.float32
+        ),
+        axis=1,
+    )
     logits = jnp.dot(normed_rows, router_full, preferred_element_type=jnp.float32)
     chosen = jnp.take_along_axis(logits, route_ids, axis=1)
     raised = jnp.exp(chosen)
     gates = raised / jnp.sum(raised, axis=1, keepdims=True)
     gate_slot = jnp.sum(jnp.where(slot_hit, gates[:, :, None], 0.0), axis=1)
-    combined = jnp.dot(
+    moe_sum = jnp.dot(
         gate_slot,
-        returned.reshape(expert_count * capacity, model_width).astype(jnp.float32),
+        expert_parts.reshape(expert_count * capacity, feat_part),
         precision=lax.Precision.HIGHEST,
         preferred_element_type=jnp.float32,
     )
-    moe_sum = lax.psum_scatter(combined, "tp", scatter_dimension=1, tiled=True)
     moe_out = jnp.where(live, moe_sum, 0.0).astype(jnp.bfloat16)
     return (attn_out, moe_out)
 

time: 510 us -> 488 us (0.957)
  waiting for transfers between devices: 201 us -> 168 us
  local copies, waits for them, and re-layouts: 30.9 us -> 41.2 us
  matrix products: 33.3 us -> 27.8 us
    unnamed x5 -> x3, waiting for transfers between devices: 82 us -> 40.2 us
    reshape x0 -> x2, local copies, waits for them, and re-layouts: none -> 16 us  [local(): results.reshape(req_count, item_count, tp_count, feat_part)]
    all_gather x1, waiting for transfers between devices: 22 us -> 27.8 us  [local(): shard_rows = lax.all_gather(prefix_cache, 'req', axis=0, tiled=True)]
    dot_general x1, matrix products: 8.25 us -> 2.66 us  [local(): jnp.dot(gate_slot, expert_parts.reshape(expert_count * capacity, feat_par...]
  transfers between devices with their start and end apart: 4 -> 3, of which waited for: 4 -> 3; matrix products, arithmetic and copies ran while one was open for 7% -> 7% of each run, Pallas kernels for 0% -> 0%
where the time goes in v7:
time: 488 us; the launch traced here: 485 us
  waiting for transfers between devices  168 us (34%)
  blocking collectives  163 us (33%)
  local copies, waits for them, and re-layouts  41.2 us (8%)
  Pallas kernels  36.8 us (8%)
  matrix products  27.8 us (6%)
  starting transfers between devices  22.2 us (5%)
  between operations  14.4 us (3%)
  other arithmetic  11.7 us (2%)
    all_to_all x1, waiting for transfers between devices, local(): lax.all_to_all(send_results, ('req', 'tp'), split_axis=0, concat_axis=0,...  100 us
    all_to_all x1, blocking collectives, local(): lax.all_to_all(picked_rows.reshape(expert_count, capacity, normed_rows.sh...  98.3 us
    unnamed x3, waiting for transfers between devices  40.2 us
    pallas_call x1, Pallas kernels, prefix_attention(): pl.pallas_call(kernel, out_shape=jax.ShapeDtypeStruct((rows, width), jnp....  36.8 us
    all_gather x1, blocking collectives, local(): gathered = lax.all_gather(packed, 'tp', axis=0, tiled=True)  34.9 us
    all_gather x1, blocking collectives, local(): resid_rows = lax.all_gather(resid, 'tp', axis=1, tiled=True)  29.6 us
    all_gather x1, waiting for transfers between devices, local(): shard_rows = lax.all_gather(prefix_cache, 'req', axis=0, tiled=True)  27.8 us
    all_to_all x1, starting transfers between devices, local(): lax.all_to_all(send_results, ('req', 'tp'), split_axis=0, concat_axis=0,...  22.1 us
  transfers between devices with their start and end apart: 3, of which 3 were waited for; matrix products, arithmetic and copies ran while one was open for 7% of the time, Pallas kernels for 0%

profile of v7, /device:TPU:8, one launch (start us, length us, event | category | flops | bytes accessed | tf_op | source)
XLA Modules:
  0.0 485.1 jit_solution(7497265199033892309)
XLA Ops:
  9.8 34.9 %all-gather = bf16[8,360,160]{1,2,0:T(8,128)(2,1)S(1)} all-gather(bf16[1,360,160]{1,2,0:T(8,128)(2,1)S(1)} %maximum_bitcast_fusion.1), channel_id=1, replica_groups=mesh['req'=32,'tp'=8] {'tp'}, dimensions={0}, use_global_device_ids=true | all-gather | bytes 1036800 | tf_op jit(solution)/shard_map/all_gather | solution.py:141
  46.1 2.7 reshape.372
  48.8 1.4 fusion.3
  50.4 2.4 fusion.31
  53.1 2.3 fusion.29
  57.7 4.6 copy.120
  64.9 27.8 %all-gather.3.cloned.1.call-done.kv_ref = bf16[32768,128]{1,0:T(8,128)(2,1)} async-done(((bf16[1024,128]{1,0:T(8,128)(2,1)}), bf16[32768,128]{1,0:T(8,128)(2,1)}) %all-gather.3.cloned.1.call-update) | async-done | bytes 8388624 | tf_op jit(solution)/shard_map/all_gather | solution.py:182
  92.7 36.8 %shard_map.149 = bf16[1024,128]{1,0:T(8,128)(2,1)} custom-call(s32[1]{0:T(128)} %dynamic_slice.7.group_ref, bf16[1024,128]{1,0:T(8,128)(2,1)} %concatenate.40.q_ref, bf16[32768,128]{1,0:T(8,128)(2,1)} %all-gather.3.cloned.1.call-done.kv_ref, f32[1024,1]{1,0:T(8,128)} %copy-done.2, f32[1024,1]{1,0:T(8,128)} %exponential_add_fusion.l0_ref, ...), custom_call_target="tpu_custom_call" | custom-call | flops 8589934592 | bytes 5242880 | tf_op jit(solution)/shard_map/pallas_call | solution.py:81
  130.7 5.4 %convolution_bitcast_fusion = f32[128,2880]{0,1:T(8,128)} fusion(bf16[8,128,64]{2,1,0:T(8,128)(2,1)S(1)} %bitcast.107, bf16[8,64,2880]{2,1,0:T(8,128)(2,1)} %bitcast.103), kind=kOutput, calls=%fused_computation.5 | convolution fusion | flops 377487360 | bytes 4554752 | tf_op jit(solution)/shard_map/hqd,hdo->qo/dot_general | solution.py:188
  138.7 39.5 %reduce-scatter.5.cloned.1.call-done = f32[128,360]{0,1:T(8,128)} async-done(((f32[128,2880]{0,1:T(8,128)}), f32[128,360]{0,1:T(8,128)}) %reduce-scatter.5.cloned.1.call-update) | async-done | bytes 184336
  179.1 29.6 %all_gather.11 = bf16[128,2880]{0,1:T(8,128)(2,1)S(1)} all-gather(bf16[128,360]{0,1:T(8,128)(2,1)S(1)} %add_convert_fusion), channel_id=1, replica_groups=mesh['req'=32,'tp'=8] {'tp'}, dimensions={1}, use_global_device_ids=true | all-gather | bytes 829440 | tf_op jit(solution)/shard_map/all_gather | solution.py:214
  209.1 3.8 convolution_convert_fusion.1
  212.9 6.5 %copy.128 = bf16[768,2880]{1,0:T(8,128)(2,1)} copy(bf16[768,2880]{0,1:T(8,128)(2,1)} %convolution_convert_fusion.1) | data formatting | bytes 8847360 | tf_op jit(solution)/shard_map/convert_element_type | solution.py:223
  219.4 98.3 %all_to_all.10 = bf16[32,24,2880]{2,1,0:T(8,128)(2,1)S(1)} all-to-all(bf16[32,24,2880]{2,1,0:T(8,128)(2,1)} %bitcast.101), channel_id=1, replica_groups=mesh['req'=32,'tp'=8] {'req'}, dimensions={0} | all-to-all | bytes 8847360 | tf_op jit(solution)/shard_map/all_to_all | solution.py:224
  317.8 3.8 convolution_bitcast_fusion.1
  321.6 4.5 fusion
  326.1 10.6 %reshape.356 = bf16[32,24,8,360]{3,2,1,0:T(8,128)(2,1)} reshape(bf16[32,1,24,2880]{3,2,0,1:T(8,128)(2,1)} %fusion) | data formatting | bytes 8847360 | tf_op jit(solution)/shard_map/reshape | solution.py:247
  336.6 5.4 %copy.129 = bf16[32,24,8,360]{3,1,2,0:T(8,128)(2,1)} copy(bf16[32,24,8,360]{3,2,1,0:T(8,128)(2,1)} %reshape.356) | data formatting | bytes 8847360 | tf_op jit(solution)/shard_map/reshape | solution.py:247
  342.1 22.1 %all-to-all-start.1 = ((bf16[256,24,360]{2,1,0:T(8,128)(2,1)}), bf16[256,24,360]{2,1,0:T(8,128)(2,1)}, u32[]{:S(2)}, u32[]{:S(2)}) async-start(bf16[256,24,360]{2,1,0:T(8,128)(2,1)} %bitcast.100), calls=%async_computation.1 | async-start | bytes 9437184 | tf_op jit(solution)/shard_map/all_to_all | solution.py:251
  365.7 1.5 fusion.26
  367.2 3.7 gather_fusion
  372.1 100.0 %all-to-all-done.1 = bf16[256,24,360]{2,1,0:T(8,128)(2,1)} async-done(((bf16[256,24,360]{2,1,0:T(8,128)(2,1)}), bf16[256,24,360]{2,1,0:T(8,128)(2,1)}, u32[]{:S(2)}, u32[]{:S(2)}) %all-to-all-start.1) | async-done | bytes 4423712 | tf_op jit(solution)/shard_map/all_to_all | solution.py:251
  472.1 3.4 convert_reduce_fusion
  475.5 2.7 fusion.14
  (87 shorter events, 16.7 us)
Async XLA Ops:
  7.2 43.2 %copy-start = (bf16[2880,512]{1,0:T(8,128)(2,1)S(1)}, bf16[2880,512]{1,0:T(8,128)(2,1)}, u32[]{:S(2)}) copy-start(bf16[2880,512]{1,0:T(8,128)(2,1)} %param.16) | copy-start | bytes 8847364
  7.2 85.5 %all-gather.3.cloned.1.call-start = ((), (), s32[]{:S(2)}) async-start(), calls=%async_computation.3 | async-start | bytes 8650752 | tf_op jit(solution)/shard_map/all_gather | solution.py:182
  7.9 170.3 %reduce-scatter.5.cloned.1.call-start = ((), (), s32[]{:S(2)}) async-start(), calls=%async_computation.4 | async-start | bytes 1658880
  46.1 4.2 copy-start.9
  53.1 2.8 copy-start.7
  56.8 7.2 %copy-start.2 = (f32[1024,1]{1,0:T(8,128)}, f32[1024,1]{1,0:T(8,128)S(1)}, u32[]{:S(2)}) copy-start(f32[1024,1]{1,0:T(8,128)S(1)} %copy.119.m0_ref) | copy-start | bytes 12292
  57.7 4.6 copy-start.10
  130.7 5.4 %copy-start.5 = (s32[128,4]{0,1:T(4,128)S(1)}, s32[128,4]{0,1:T(4,128)}, u32[]{:S(2)}) copy-start(s32[128,4]{0,1:T(4,128)} %param.25) | copy-start | bytes 6148
  136.1 42.1 %copy-start.4 = (bf16[128,360]{0,1:T(8,128)(2,1)S(1)}, bf16[128,360]{0,1:T(8,128)(2,1)}, u32[]{:S(2)}) copy-start(bf16[128,360]{0,1:T(8,128)(2,1)} %param.14) | copy-start | bytes 276484
  136.1 73.0 %copy-start.6 = (f32[2880]{0:T(1024)S(1)}, f32[2880]{0:T(1024)}, u32[]{:S(2)}) copy-start(f32[2880]{0:T(1024)} %param.21) | copy-start | bytes 34564
  212.9 104.8 %slice-start = ((s8[4239360]{0:T(1024)(128)(4,1)}), s8[45056]{0:T(1024)(128)(4,1)S(1)}, s32[]{:S(2)}) async-start(s8[4239360]{0:T(1024)(128)(4,1)} %bitcast.115), calls=%async_computation.5 | async-start | bytes 90112
  219.4 98.3 %slice-start.1 = ((s8[4239360]{0:T(1024)(128)(4,1)}), s8[4194304]{0:T(1024)(128)(4,1)S(1)}, s32[]{:S(2)}) async-start(s8[4239360]{0:T(1024)(128)(4,1)} %bitcast.115), calls=%async_computation.6 | async-start | bytes 8388608
  317.8 3.9 copy-start.8
  342.1 22.4 %copy-start.11 = (s32[32]{0:T(128)S(1)}, s32[32]{0:T(128)}, u32[]{:S(2)}) copy-start(s32[32]{0:T(128)} %param.27) | copy-start | bytes 388
  342.1 130.0 %all-to-all-start.1 = ((bf16[256,24,360]{2,1,0:T(8,128)(2,1)}), bf16[256,24,360]{2,1,0:T(8,128)(2,1)}, u32[]{:S(2)}, u32[]{:S(2)}) async-start(bf16[256,24,360]{2,1,0:T(8,128)(2,1)} %bitcast.100), calls=%async_computation.1 | async-start | bytes 9437184 | tf_op jit(solution)/shard_map/all_to_all | solution.py:251
  367.2 4.2 copy-start.3
  472.1 6.1 %copy-start.1 = (bf16[2880,512]{1,0:T(8,128)(2,1)S(1)}, bf16[2880,512]{1,0:T(8,128)(2,1)}, u32[]{:S(2)}) copy-start(bf16[2880,512]{1,0:T(8,128)(2,1)} %param.16) | copy-start | bytes 8847364
Sparse Core Ops, SparseCore 0:
  10.6 82.1 all-gather.2
  136.2 41.9 reduce-scatter.4

commit v8 on v7

--- a/solution.py
+++ b/solution.py
@@ -238,16 +238,14 @@
     active = ((up_value + 1.0) * gate_value * jax.nn.sigmoid(glu_alpha * gate_value)).astype(
         jnp.bfloat16
     )
-    results = jnp.einsum(
-        "sepf,efd->sepd", active, down_weight, preferred_element_type=jnp.float32
-    ).astype(jnp.bfloat16)
     tp_count = lax.axis_size("tp")
     feat_part = model_width // tp_count
-    send_results = (
-        results.reshape(req_count, item_count, tp_count, feat_part)
-        .transpose(0, 2, 1, 3)
-        .reshape(req_count * tp_count, item_count, feat_part)
-    )
+    send_results = jnp.einsum(
+        "sepf,eftd->setpd",
+        active,
+        down_weight.reshape(exp_local, ff_local, tp_count, feat_part),
+        preferred_element_type=jnp.float32,
+    ).astype(jnp.bfloat16).reshape(req_count * exp_local * tp_count, item_count, feat_part)
     returned = lax.all_to_all(
         send_results, ("req", "tp"), split_axis=0, concat_axis=0, tiled=True
     )

time: 488 us -> 477 us (0.977)
  blocking collectives: 163 us -> 64.5 us
  waiting for transfers between devices: 168 us -> 246 us
  starting transfers between devices: 22.2 us -> 31.9 us
  local copies, waits for them, and re-layouts: 41.2 us -> 36.2 us
    all_to_all x1 -> x0, blocking collectives: 98.3 us -> none  [local(): lax.all_to_all(picked_rows.reshape(expert_count, capacity, normed_rows.sh...]
    all_to_all x0 -> x1, waiting for transfers between devices: none -> 83.7 us  [local(): lax.all_to_all(picked_rows.reshape(expert_count, capacity, normed_rows.sh...]
    reshape x2 -> x0, local copies, waits for them, and re-layouts: 16 us -> none  [local(): results.reshape(req_count, item_count, tp_count, feat_part)]
    all_to_all x0 -> x1, starting transfers between devices: none -> 9.46 us  [local(): lax.all_to_all(picked_rows.reshape(expert_count, capacity, normed_rows.sh...]
    all_gather x1, waiting for transfers between devices: 27.8 us -> 22 us  [local(): shard_rows = lax.all_gather(prefix_cache, 'req', axis=0, tiled=True)]
    another operation x1 -> x2, local copies, waits for them, and re-layouts: 0.01 us -> 5.57 us
  transfers between devices with their start and end apart: 3 -> 4, of which waited for: 3 -> 4; matrix products, arithmetic and copies ran while one was open for 7% -> 9% of each run, Pallas kernels for 0% -> 0%
where the time goes in v8:
time: 477 us; the launch traced here: 474 us
  waiting for transfers between devices  246 us (52%)
  blocking collectives  64.5 us (14%)
  Pallas kernels  36.9 us (8%)
  local copies, waits for them, and re-layouts  36.2 us (8%)
  starting transfers between devices  31.9 us (7%)
  matrix products  31.2 us (7%)
  between operations  14.4 us (3%)
  other arithmetic  13 us (3%)
    all_to_all x1, waiting for transfers between devices, local(): lax.all_to_all(send_results, ('req', 'tp'), split_axis=0, concat_axis=0,...  99.7 us
    all_to_all x1, waiting for transfers between devices, local(): lax.all_to_all(picked_rows.reshape(expert_count, capacity, normed_rows.sh...  83.7 us
    unnamed x3, waiting for transfers between devices  40.2 us
    pallas_call x1, Pallas kernels, prefix_attention(): pl.pallas_call(kernel, out_shape=jax.ShapeDtypeStruct((rows, width), jnp....  36.9 us
    all_gather x1, blocking collectives, local(): gathered = lax.all_gather(packed, 'tp', axis=0, tiled=True)  34.9 us
    all_gather x1, blocking collectives, local(): resid_rows = lax.all_gather(resid, 'tp', axis=1, tiled=True)  29.5 us
    all_to_all x1, starting transfers between devices, local(): lax.all_to_all(send_results, ('req', 'tp'), split_axis=0, concat_axis=0,...  22.4 us
    all_gather x1, waiting for transfers between devices, local(): shard_rows = lax.all_gather(prefix_cache, 'req', axis=0, tiled=True)  22 us
  transfers between devices with their start and end apart: 4, of which 4 were waited for; matrix products, arithmetic and copies ran while one was open for 9% of the time, Pallas kernels for 0%

profile of v8, /device:TPU:8, one launch (start us, length us, event | category | flops | bytes accessed | tf_op | source)
XLA Modules:
  0.0 473.6 jit_solution(9063515897688192157)
XLA Ops:
  9.8 34.9 %all-gather = bf16[8,360,160]{1,2,0:T(8,128)(2,1)S(1)} all-gather(bf16[1,360,160]{1,2,0:T(8,128)(2,1)S(1)} %maximum_bitcast_fusion.1), channel_id=1, replica_groups=mesh['req'=32,'tp'=8] {'tp'}, dimensions={0}, use_global_device_ids=true | all-gather | bytes 1036800 | tf_op jit(solution)/shard_map/all_gather | solution.py:141
  46.1 2.7 reshape.370
  50.4 2.4 fusion.31
  53.8 1.9 fusion.29
  61.4 4.7 copy.121
  68.5 2.3 exponential_add_fusion.l0_ref
  70.8 22.0 %all-gather.3.cloned.1.call-done.kv_ref = bf16[32768,128]{1,0:T(8,128)(2,1)} async-done(((bf16[1024,128]{1,0:T(8,128)(2,1)}), bf16[32768,128]{1,0:T(8,128)(2,1)}) %all-gather.3.cloned.1.call-update) | async-done | bytes 8388624 | tf_op jit(solution)/shard_map/all_gather | solution.py:182
  92.8 36.9 %shard_map.149 = bf16[1024,128]{1,0:T(8,128)(2,1)} custom-call(s32[1]{0:T(128)} %dynamic_slice.7.group_ref, bf16[1024,128]{1,0:T(8,128)(2,1)} %concatenate.40.q_ref, bf16[32768,128]{1,0:T(8,128)(2,1)} %all-gather.3.cloned.1.call-done.kv_ref, f32[1024,1]{1,0:T(8,128)} %copy.120.m0_ref, f32[1024,1]{1,0:T(8,128)} %exponential_add_fusion.l0_ref, ...), custom_call_target="tpu_custom_call" | custom-call | flops 8589934592 | bytes 5242880 | tf_op jit(solution)/shard_map/pallas_call | solution.py:81
  130.7 5.4 %convolution_bitcast_fusion = f32[128,2880]{0,1:T(8,128)} fusion(bf16[8,128,64]{2,1,0:T(8,128)(2,1)S(1)} %bitcast.103, bf16[8,64,2880]{2,1,0:T(8,128)(2,1)} %bitcast.99), kind=kOutput, calls=%fused_computation.3 | convolution fusion | flops 377487360 | bytes 4554752 | tf_op jit(solution)/shard_map/hqd,hdo->qo/dot_general | solution.py:188
  138.7 39.5 %reduce-scatter.5.cloned.1.call-done = f32[128,360]{0,1:T(8,128)} async-done(((f32[128,2880]{0,1:T(8,128)}), f32[128,360]{0,1:T(8,128)}) %reduce-scatter.5.cloned.1.call-update) | async-done | bytes 184336
  179.2 29.5 %all_gather.11 = bf16[128,2880]{0,1:T(8,128)(2,1)S(1)} all-gather(bf16[128,360]{0,1:T(8,128)(2,1)S(1)} %add_convert_fusion), channel_id=1, replica_groups=mesh['req'=32,'tp'=8] {'tp'}, dimensions={1}, use_global_device_ids=true | all-gather | bytes 829440 | tf_op jit(solution)/shard_map/all_gather | solution.py:214
  209.6 3.8 convolution_convert_fusion
  213.4 6.5 %copy.129 = bf16[768,2880]{1,0:T(8,128)(2,1)} copy(bf16[768,2880]{0,1:T(8,128)(2,1)} %convolution_convert_fusion) | data formatting | bytes 8847360 | tf_op jit(solution)/shard_map/convert_element_type | solution.py:223
  219.9 9.5 %all-to-all-start = ((bf16[32,24,2880]{2,1,0:T(8,128)(2,1)}), bf16[32,24,2880]{2,1,0:T(8,128)(2,1)}, u32[]{:S(2)}, u32[]{:S(2)}) async-start(bf16[32,24,2880]{2,1,0:T(8,128)(2,1)} %bitcast.96), calls=%async_computation | async-start | bytes 9043968 | tf_op jit(solution)/shard_map/all_to_all | solution.py:224
  229.3 5.6 %reshape.354 = bf16[360,8,360]{2,1,0:T(8,128)(2,1)} reshape(bf16[1,360,2880]{2,1,0:T(8,128)(2,1)} %param.24) | data formatting | bytes 4147200 | tf_op jit(solution)/shard_map/reshape.10
  234.9 83.7 %all-to-all-done = bf16[32,24,2880]{2,1,0:T(8,128)(2,1)} async-done(((bf16[32,24,2880]{2,1,0:T(8,128)(2,1)}), bf16[32,24,2880]{2,1,0:T(8,128)(2,1)}, u32[]{:S(2)}, u32[]{:S(2)}) %all-to-all-start) | async-done | bytes 4423712 | tf_op jit(solution)/shard_map/all_to_all | solution.py:224
  318.6 7.1 %convolution_bitcast_fusion.1 = f32[32,1,24,720]{3,2,0,1:T(8,128)S(1)} fusion(bf16[32,24,2880]{2,1,0:T(8,128)(2,1)} %all-to-all-done, bf16[2880,720,1]{0,1,2:T(8,128)(2,1)} %bitcast.111), kind=kOutput, calls=%fused_computation.11 | convolution fusion | flops 3185049600 | bytes 10782720 | tf_op jit(solution)/shard_map/sepd,edf->sepf/dot_general | solution.py:233
  325.7 4.8 %convolution_convert_fusion.1 = bf16[32,24,8,360]{3,1,2,0:T(8,128)(2,1)} fusion(bf16[360,8,360]{2,1,0:T(8,128)(2,1)S(1)} %copy-done.3, f32[32,1,24,720]{3,2,0,1:T(8,128)S(1)} %convolution_bitcast_fusion.1), kind=kOutput, calls=%fused_computation.4 | convolution fusion | flops 1597501440 | bytes 8709120 | tf_op jit(solution)/shard_map/sepf,eftd->setpd/dot_general | solution.py:243
  330.5 22.4 %all-to-all-start.1 = ((bf16[256,24,360]{2,1,0:T(8,128)(2,1)}), bf16[256,24,360]{2,1,0:T(8,128)(2,1)}, u32[]{:S(2)}, u32[]{:S(2)}) async-start(bf16[256,24,360]{2,1,0:T(8,128)(2,1)} %bitcast.97), calls=%async_computation.1 | async-start | bytes 9437184 | tf_op jit(solution)/shard_map/all_to_all | solution.py:249
  354.4 1.8 fusion.26
  356.2 3.7 gather_fusion
  361.1 99.7 %all-to-all-done.1 = bf16[256,24,360]{2,1,0:T(8,128)(2,1)} async-done(((bf16[256,24,360]{2,1,0:T(8,128)(2,1)}), bf16[256,24,360]{2,1,0:T(8,128)(2,1)}, u32[]{:S(2)}, u32[]{:S(2)}) %all-to-all-start.1) | async-done | bytes 4423712 | tf_op jit(solution)/shard_map/all_to_all | solution.py:249
  460.9 3.3 convert_reduce_fusion
  464.1 2.7 fusion.14
  (84 shorter events, 22.6 us)
Async XLA Ops:
  7.2 43.2 %copy-start = (bf16[2880,512]{1,0:T(8,128)(2,1)S(1)}, bf16[2880,512]{1,0:T(8,128)(2,1)}, u32[]{:S(2)}) copy-start(bf16[2880,512]{1,0:T(8,128)(2,1)} %param.16) | copy-start | bytes 8847364
  7.2 85.6 %all-gather.3.cloned.1.call-start = ((), (), s32[]{:S(2)}) async-start(), calls=%async_computation.3 | async-start | bytes 8650752 | tf_op jit(solution)/shard_map/all_gather | solution.py:182
  7.9 170.3 %reduce-scatter.5.cloned.1.call-start = ((), (), s32[]{:S(2)}) async-start(), calls=%async_computation.4 | async-start | bytes 1658880
  46.1 4.2 copy-start.10
  53.8 2.1 copy-start.2
  53.8 2.5 copy-start.9
  55.6 0.6 copy-start.7
  61.4 4.7 copy-start.11
  130.7 5.4 %copy-start.6 = (s32[128,4]{0,1:T(4,128)S(1)}, s32[128,4]{0,1:T(4,128)}, u32[]{:S(2)}) copy-start(s32[128,4]{0,1:T(4,128)} %param.25) | copy-start | bytes 6148
  136.1 42.1 %copy-start.5 = (bf16[128,360]{0,1:T(8,128)(2,1)S(1)}, bf16[128,360]{0,1:T(8,128)(2,1)}, u32[]{:S(2)}) copy-start(bf16[128,360]{0,1:T(8,128)(2,1)} %param.14) | copy-start | bytes 276484
  136.2 73.4 %copy-start.8 = (f32[2880]{0:T(1024)S(1)}, f32[2880]{0:T(1024)}, u32[]{:S(2)}) copy-start(f32[2880]{0:T(1024)} %param.21) | copy-start | bytes 34564
  208.7 0.9 copy-start.1
  219.9 98.7 %all-to-all-start = ((bf16[32,24,2880]{2,1,0:T(8,128)(2,1)}), bf16[32,24,2880]{2,1,0:T(8,128)(2,1)}, u32[]{:S(2)}, u32[]{:S(2)}) async-start(bf16[32,24,2880]{2,1,0:T(8,128)(2,1)} %bitcast.96), calls=%async_computation | async-start | bytes 9043968 | tf_op jit(solution)/shard_map/all_to_all | solution.py:224
  318.6 7.1 %copy-start.3 = (bf16[360,8,360]{2,1,0:T(8,128)(2,1)S(1)}, bf16[360,8,360]{2,1,0:T(8,128)(2,1)}, u32[]{:S(2)}) copy-start(bf16[360,8,360]{2,1,0:T(8,128)(2,1)} %reshape.354) | copy-start | bytes 6220804
  330.5 22.6 %copy-start.12 = (s32[32]{0:T(128)S(1)}, s32[32]{0:T(128)}, u32[]{:S(2)}) copy-start(s32[32]{0:T(128)} %param.27) | copy-start | bytes 388
  330.5 130.3 %all-to-all-start.1 = ((bf16[256,24,360]{2,1,0:T(8,128)(2,1)}), bf16[256,24,360]{2,1,0:T(8,128)(2,1)}, u32[]{:S(2)}, u32[]{:S(2)}) async-start(bf16[256,24,360]{2,1,0:T(8,128)(2,1)} %bitcast.97), calls=%async_computation.1 | async-start | bytes 9437184 | tf_op jit(solution)/shard_map/all_to_all | solution.py:249
  356.2 4.2 copy-start.4
Sparse Core Ops, SparseCore 0:
  10.6 82.1 all-gather.2
  136.3 41.8 reduce-scatter.4

commit v9 on v8

--- a/solution.py
+++ b/solution.py
@@ -74,7 +74,7 @@
 def prefix_attention(group, query, cache, peak, denominator, accum, *, prefix_len, scale):
     rows, width = query.shape
     block_q = min(rows, 1024)
-    block_k = 2048
+    block_k = 4096
     steps = prefix_len // block_k
     grid = (rows // block_q, steps)
     kernel = functools.partial(flash_kernel, scale=scale, steps=steps)

time: 477 us -> 475 us (level)
  waiting for transfers between devices: 246 us -> 260 us
  starting transfers between devices: 31.9 us -> 19 us
    all_to_all x1, waiting for transfers between devices: 83.7 us -> 98 us  [local(): lax.all_to_all(picked_rows.reshape(expert_count, capacity, normed_rows.sh...]
    all_to_all x1, starting transfers between devices: 22.4 us -> 9.59 us  [local(): lax.all_to_all(send_results, ('req', 'tp'), split_axis=0, concat_axis=0,...]
where the time goes in v9:
time: 475 us; the launch traced here: 472 us
  waiting for transfers between devices  260 us (55%)
  blocking collectives  64.5 us (14%)
  local copies, waits for them, and re-layouts  36.2 us (8%)
  Pallas kernels  33.9 us (7%)
  matrix products  31.2 us (7%)
  starting transfers between devices  19 us (4%)
  between operations  14.3 us (3%)
  other arithmetic  12.8 us (3%)
    all_to_all x1, waiting for transfers between devices, local(): lax.all_to_all(send_results, ('req', 'tp'), split_axis=0, concat_axis=0,...  99.8 us
    all_to_all x1, waiting for transfers between devices, local(): lax.all_to_all(picked_rows.reshape(expert_count, capacity, normed_rows.sh...  98 us
    unnamed x3, waiting for transfers between devices  40.3 us
    all_gather x1, blocking collectives, local(): gathered = lax.all_gather(packed, 'tp', axis=0, tiled=True)  34.9 us
    pallas_call x1, Pallas kernels, prefix_attention(): pl.pallas_call(kernel, out_shape=jax.ShapeDtypeStruct((rows, width), jnp....  33.9 us
    all_gather x1, blocking collectives, local(): resid_rows = lax.all_gather(resid, 'tp', axis=1, tiled=True)  29.6 us
    all_gather x1, waiting for transfers between devices, local(): shard_rows = lax.all_gather(prefix_cache, 'req', axis=0, tiled=True)  22 us
    all_to_all x1, starting transfers between devices, local(): lax.all_to_all(send_results, ('req', 'tp'), split_axis=0, concat_axis=0,...  9.59 us
  transfers between devices with their start and end apart: 4, of which 4 were waited for; matrix products, arithmetic and copies ran while one was open for 9% of the time, Pallas kernels for 0%

profile of v9, /device:TPU:8, one launch (start us, length us, event | category | flops | bytes accessed | tf_op | source)
XLA Modules:
  0.0 472.1 jit_solution(15060952931736564044)
XLA Ops:
  9.8 34.9 %all-gather = bf16[8,360,160]{1,2,0:T(8,128)(2,1)S(1)} all-gather(bf16[1,360,160]{1,2,0:T(8,128)(2,1)S(1)} %maximum_bitcast_fusion.1), channel_id=1, replica_groups=mesh['req'=32,'tp'=8] {'tp'}, dimensions={0}, use_global_device_ids=true | all-gather | bytes 1036800 | tf_op jit(solution)/shard_map/all_gather | solution.py:141
  46.1 2.7 reshape.370
  50.4 2.4 fusion.31
  53.8 1.9 fusion.29
  61.4 4.7 copy.121
  68.5 2.3 exponential_add_fusion.l0_ref
  70.8 22.0 %all-gather.3.cloned.1.call-done.kv_ref = bf16[32768,128]{1,0:T(8,128)(2,1)} async-done(((bf16[1024,128]{1,0:T(8,128)(2,1)}), bf16[32768,128]{1,0:T(8,128)(2,1)}) %all-gather.3.cloned.1.call-update) | async-done | bytes 8388624 | tf_op jit(solution)/shard_map/all_gather | solution.py:182
  92.8 33.9 %shard_map.149 = bf16[1024,128]{1,0:T(8,128)(2,1)} custom-call(s32[1]{0:T(128)} %dynamic_slice.7.group_ref, bf16[1024,128]{1,0:T(8,128)(2,1)} %concatenate.40.q_ref, bf16[32768,128]{1,0:T(8,128)(2,1)} %all-gather.3.cloned.1.call-done.kv_ref, f32[1024,1]{1,0:T(8,128)} %copy.120.m0_ref, f32[1024,1]{1,0:T(8,128)} %exponential_add_fusion.l0_ref, ...), custom_call_target="tpu_custom_call" | custom-call | flops 8589934592 | bytes 5242880 | tf_op jit(solution)/shard_map/pallas_call | solution.py:81
  127.8 5.4 %convolution_bitcast_fusion = f32[128,2880]{0,1:T(8,128)} fusion(bf16[8,128,64]{2,1,0:T(8,128)(2,1)S(1)} %bitcast.103, bf16[8,64,2880]{2,1,0:T(8,128)(2,1)} %bitcast.99), kind=kOutput, calls=%fused_computation.3 | convolution fusion | flops 377487360 | bytes 4554752 | tf_op jit(solution)/shard_map/hqd,hdo->qo/dot_general | solution.py:188
  135.6 39.6 %reduce-scatter.5.cloned.1.call-done = f32[128,360]{0,1:T(8,128)} async-done(((f32[128,2880]{0,1:T(8,128)}), f32[128,360]{0,1:T(8,128)}) %reduce-scatter.5.cloned.1.call-update) | async-done | bytes 184336
  176.1 29.6 %all_gather.11 = bf16[128,2880]{0,1:T(8,128)(2,1)S(1)} all-gather(bf16[128,360]{0,1:T(8,128)(2,1)S(1)} %add_convert_fusion), channel_id=1, replica_groups=mesh['req'=32,'tp'=8] {'tp'}, dimensions={1}, use_global_device_ids=true | all-gather | bytes 829440 | tf_op jit(solution)/shard_map/all_gather | solution.py:214
  206.6 3.8 convolution_convert_fusion
  210.4 6.5 %copy.129 = bf16[768,2880]{1,0:T(8,128)(2,1)} copy(bf16[768,2880]{0,1:T(8,128)(2,1)} %convolution_convert_fusion) | data formatting | bytes 8847360 | tf_op jit(solution)/shard_map/convert_element_type | solution.py:223
  216.9 9.3 %all-to-all-start = ((bf16[32,24,2880]{2,1,0:T(8,128)(2,1)}), bf16[32,24,2880]{2,1,0:T(8,128)(2,1)}, u32[]{:S(2)}, u32[]{:S(2)}) async-start(bf16[32,24,2880]{2,1,0:T(8,128)(2,1)} %bitcast.96), calls=%async_computation | async-start | bytes 9043968 | tf_op jit(solution)/shard_map/all_to_all | solution.py:224
  226.3 5.6 %reshape.354 = bf16[360,8,360]{2,1,0:T(8,128)(2,1)} reshape(bf16[1,360,2880]{2,1,0:T(8,128)(2,1)} %param.24) | data formatting | bytes 4147200 | tf_op jit(solution)/shard_map/reshape.10
  231.8 98.0 %all-to-all-done = bf16[32,24,2880]{2,1,0:T(8,128)(2,1)} async-done(((bf16[32,24,2880]{2,1,0:T(8,128)(2,1)}), bf16[32,24,2880]{2,1,0:T(8,128)(2,1)}, u32[]{:S(2)}, u32[]{:S(2)}) %all-to-all-start) | async-done | bytes 4423712 | tf_op jit(solution)/shard_map/all_to_all | solution.py:224
  329.8 7.1 %convolution_bitcast_fusion.1 = f32[32,1,24,720]{3,2,0,1:T(8,128)S(1)} fusion(bf16[32,24,2880]{2,1,0:T(8,128)(2,1)} %all-to-all-done, bf16[2880,720,1]{0,1,2:T(8,128)(2,1)} %bitcast.111), kind=kOutput, calls=%fused_computation.11 | convolution fusion | flops 3185049600 | bytes 10782720 | tf_op jit(solution)/shard_map/sepd,edf->sepf/dot_general | solution.py:233
  336.9 4.8 %convolution_convert_fusion.1 = bf16[32,24,8,360]{3,1,2,0:T(8,128)(2,1)} fusion(bf16[360,8,360]{2,1,0:T(8,128)(2,1)S(1)} %copy-done.3, f32[32,1,24,720]{3,2,0,1:T(8,128)S(1)} %convolution_bitcast_fusion.1), kind=kOutput, calls=%fused_computation.4 | convolution fusion | flops 1597501440 | bytes 8709120 | tf_op jit(solution)/shard_map/sepf,eftd->setpd/dot_general | solution.py:243
  341.8 9.6 %all-to-all-start.1 = ((bf16[256,24,360]{2,1,0:T(8,128)(2,1)}), bf16[256,24,360]{2,1,0:T(8,128)(2,1)}, u32[]{:S(2)}, u32[]{:S(2)}) async-start(bf16[256,24,360]{2,1,0:T(8,128)(2,1)} %bitcast.97), calls=%async_computation.1 | async-start | bytes 9437184 | tf_op jit(solution)/shard_map/all_to_all | solution.py:249
  352.8 1.8 fusion.26
  354.6 3.7 gather_fusion
  359.5 99.8 %all-to-all-done.1 = bf16[256,24,360]{2,1,0:T(8,128)(2,1)} async-done(((bf16[256,24,360]{2,1,0:T(8,128)(2,1)}), bf16[256,24,360]{2,1,0:T(8,128)(2,1)}, u32[]{:S(2)}, u32[]{:S(2)}) %all-to-all-start.1) | async-done | bytes 4423712 | tf_op jit(solution)/shard_map/all_to_all | solution.py:249
  459.3 3.3 convert_reduce_fusion
  462.6 2.7 fusion.14
  (84 shorter events, 22.4 us)
Async XLA Ops:
  7.2 43.2 %copy-start = (bf16[2880,512]{1,0:T(8,128)(2,1)S(1)}, bf16[2880,512]{1,0:T(8,128)(2,1)}, u32[]{:S(2)}) copy-start(bf16[2880,512]{1,0:T(8,128)(2,1)} %param.16) | copy-start | bytes 8847364
  7.2 85.6 %all-gather.3.cloned.1.call-start = ((), (), s32[]{:S(2)}) async-start(), calls=%async_computation.3 | async-start | bytes 8650752 | tf_op jit(solution)/shard_map/all_gather | solution.py:182
  7.9 167.3 %reduce-scatter.5.cloned.1.call-start = ((), (), s32[]{:S(2)}) async-start(), calls=%async_computation.4 | async-start | bytes 1658880
  46.1 4.2 copy-start.10
  53.8 2.1 copy-start.2
  53.8 2.5 copy-start.9
  55.6 0.6 copy-start.7
  61.4 4.7 copy-start.11
  127.7 5.4 %copy-start.6 = (s32[128,4]{0,1:T(4,128)S(1)}, s32[128,4]{0,1:T(4,128)}, u32[]{:S(2)}) copy-start(s32[128,4]{0,1:T(4,128)} %param.25) | copy-start | bytes 6148
  133.2 42.0 %copy-start.5 = (bf16[128,360]{0,1:T(8,128)(2,1)S(1)}, bf16[128,360]{0,1:T(8,128)(2,1)}, u32[]{:S(2)}) copy-start(bf16[128,360]{0,1:T(8,128)(2,1)} %param.14) | copy-start | bytes 276484
  133.2 73.4 %copy-start.8 = (f32[2880]{0:T(1024)S(1)}, f32[2880]{0:T(1024)}, u32[]{:S(2)}) copy-start(f32[2880]{0:T(1024)} %param.21) | copy-start | bytes 34564
  205.7 0.9 copy-start.1
  216.9 112.9 %all-to-all-start = ((bf16[32,24,2880]{2,1,0:T(8,128)(2,1)}), bf16[32,24,2880]{2,1,0:T(8,128)(2,1)}, u32[]{:S(2)}, u32[]{:S(2)}) async-start(bf16[32,24,2880]{2,1,0:T(8,128)(2,1)} %bitcast.96), calls=%async_computation | async-start | bytes 9043968 | tf_op jit(solution)/shard_map/all_to_all | solution.py:224
  329.8 7.1 %copy-start.3 = (bf16[360,8,360]{2,1,0:T(8,128)(2,1)S(1)}, bf16[360,8,360]{2,1,0:T(8,128)(2,1)}, u32[]{:S(2)}) copy-start(bf16[360,8,360]{2,1,0:T(8,128)(2,1)} %reshape.354) | copy-start | bytes 6220804
  341.8 9.8 %copy-start.12 = (s32[32]{0:T(128)S(1)}, s32[32]{0:T(128)}, u32[]{:S(2)}) copy-start(s32[32]{0:T(128)} %param.27) | copy-start | bytes 388
  341.8 117.5 %all-to-all-start.1 = ((bf16[256,24,360]{2,1,0:T(8,128)(2,1)}), bf16[256,24,360]{2,1,0:T(8,128)(2,1)}, u32[]{:S(2)}, u32[]{:S(2)}) async-start(bf16[256,24,360]{2,1,0:T(8,128)(2,1)} %bitcast.97), calls=%async_computation.1 | async-start | bytes 9437184 | tf_op jit(solution)/shard_map/all_to_all | solution.py:249
  354.6 4.2 copy-start.4
Sparse Core Ops, SparseCore 0:
  10.6 82.1 all-gather.2
  133.3 41.8 reduce-scatter.4

commit v10 on v9

--- a/solution.py
+++ b/solution.py
@@ -249,20 +249,20 @@
     returned = lax.all_to_all(
         send_results, ("req", "tp"), split_axis=0, concat_axis=0, tiled=True
     )
-    expert_parts = jnp.sum(
-        returned.reshape(req_count * exp_local, tp_count, item_count, feat_part).astype(
-            jnp.float32
-        ),
-        axis=1,
-    )
     logits = jnp.dot(normed_rows, router_full, preferred_element_type=jnp.float32)
     chosen = jnp.take_along_axis(logits, route_ids, axis=1)
     raised = jnp.exp(chosen)
     gates = raised / jnp.sum(raised, axis=1, keepdims=True)
     gate_slot = jnp.sum(jnp.where(slot_hit, gates[:, :, None], 0.0), axis=1)
+    gate_parts = jnp.broadcast_to(
+        gate_slot.reshape(token_count, req_count * exp_local, 1, item_count),
+        (token_count, req_count * exp_local, tp_count, item_count),
+    ).reshape(token_count, req_count * exp_local * tp_count * item_count)
     moe_sum = jnp.dot(
-        gate_slot,
-        expert_parts.reshape(expert_count * capacity, feat_part),
+        gate_parts,
+        returned.reshape(req_count * exp_local * tp_count * item_count, feat_part).astype(
+            jnp.float32
+        ),
         precision=lax.Precision.HIGHEST,
         preferred_element_type=jnp.float32,
     )

time: 475 us -> 477 us (level)
  waiting for transfers between devices: 260 us -> 267 us
  local copies, waits for them, and re-layouts: 36.2 us -> 30.3 us
  matrix products: 31.2 us -> 36.6 us
    all_gather x1, waiting for transfers between devices: 22 us -> 27.8 us  [local(): shard_rows = lax.all_gather(prefix_cache, 'req', axis=0, tiled=True)]
    dot_general x1, matrix products: 2.66 us -> 7.8 us  [local(): jnp.dot(gate_parts, returned.reshape(req_count * exp_local * tp_count * i...]
  transfers between devices with their start and end apart: 4 -> 4, of which waited for: 4 -> 4; matrix products, arithmetic and copies ran while one was open for 9% -> 8% of each run, Pallas kernels for 0% -> 0%
where the time goes in v10:
time: 477 us; the launch traced here: 476 us
  waiting for transfers between devices  267 us (56%)
  blocking collectives  64.2 us (13%)
  matrix products  36.6 us (8%)
  Pallas kernels  33.9 us (7%)
  local copies, waits for them, and re-layouts  30.3 us (6%)
  starting transfers between devices  21.4 us (4%)
  between operations  14.4 us (3%)
  other arithmetic  8.14 us (2%)
    all_to_all x1, waiting for transfers between devices, local(): lax.all_to_all(send_results, ('req', 'tp'), split_axis=0, concat_axis=0,...  99.9 us
    all_to_all x1, waiting for transfers between devices, local(): lax.all_to_all(picked_rows.reshape(expert_count, capacity, normed_rows.sh...  98.9 us
    unnamed x3, waiting for transfers between devices  40.6 us
    all_gather x1, blocking collectives, local(): gathered = lax.all_gather(packed, 'tp', axis=0, tiled=True)  34.9 us
    pallas_call x1, Pallas kernels, prefix_attention(): pl.pallas_call(kernel, out_shape=jax.ShapeDtypeStruct((rows, width), jnp....  33.9 us
    all_gather x1, blocking collectives, local(): resid_rows = lax.all_gather(resid, 'tp', axis=1, tiled=True)  29.3 us
    all_gather x1, waiting for transfers between devices, local(): shard_rows = lax.all_gather(prefix_cache, 'req', axis=0, tiled=True)  27.8 us
    all_to_all x1, starting transfers between devices, local(): lax.all_to_all(send_results, ('req', 'tp'), split_axis=0, concat_axis=0,...  11.9 us
  transfers between devices with their start and end apart: 4, of which 4 were waited for; matrix products, arithmetic and copies ran while one was open for 8% of the time, Pallas kernels for 0%

profile of v10, /device:TPU:8, one launch (start us, length us, event | category | flops | bytes accessed | tf_op | source)
XLA Modules:
  0.0 476.1 jit_solution(11109337914917998183)
XLA Ops:
  9.8 34.9 %all-gather = bf16[8,360,160]{1,2,0:T(8,128)(2,1)S(1)} all-gather(bf16[1,360,160]{1,2,0:T(8,128)(2,1)S(1)} %maximum_bitcast_fusion.1), channel_id=1, replica_groups=mesh['req'=32,'tp'=8] {'tp'}, dimensions={0}, use_global_device_ids=true | all-gather | bytes 1036800 | tf_op jit(solution)/shard_map/all_gather | solution.py:141
  44.8 1.4 copy.115
  46.1 2.7 reshape.372
  48.8 1.4 fusion.3
  50.4 2.4 fusion.31
  53.1 2.3 fusion.29
  57.7 4.6 copy.122
  64.9 27.8 %all-gather.3.cloned.1.call-done.kv_ref = bf16[32768,128]{1,0:T(8,128)(2,1)} async-done(((bf16[1024,128]{1,0:T(8,128)(2,1)}), bf16[32768,128]{1,0:T(8,128)(2,1)}) %all-gather.3.cloned.1.call-update) | async-done | bytes 8388624 | tf_op jit(solution)/shard_map/all_gather | solution.py:182
  92.7 33.9 %shard_map.149 = bf16[1024,128]{1,0:T(8,128)(2,1)} custom-call(s32[1]{0:T(128)} %dynamic_slice.7.group_ref, bf16[1024,128]{1,0:T(8,128)(2,1)} %concatenate.40.q_ref, bf16[32768,128]{1,0:T(8,128)(2,1)} %all-gather.3.cloned.1.call-done.kv_ref, f32[1024,1]{1,0:T(8,128)} %copy-done.2, f32[1024,1]{1,0:T(8,128)} %exponential_add_fusion.l0_ref, ...), custom_call_target="tpu_custom_call" | custom-call | flops 8589934592 | bytes 5242880 | tf_op jit(solution)/shard_map/pallas_call | solution.py:81
  127.7 5.4 %convolution_bitcast_fusion = f32[128,2880]{0,1:T(8,128)} fusion(bf16[8,128,64]{2,1,0:T(8,128)(2,1)S(1)} %bitcast.103, bf16[8,64,2880]{2,1,0:T(8,128)(2,1)} %bitcast.98), kind=kOutput, calls=%fused_computation.2 | convolution fusion | flops 377487360 | bytes 4554752 | tf_op jit(solution)/shard_map/hqd,hdo->qo/dot_general | solution.py:188
  135.5 39.9 %reduce-scatter.5.cloned.1.call-done = f32[128,360]{0,1:T(8,128)} async-done(((f32[128,2880]{0,1:T(8,128)}), f32[128,360]{0,1:T(8,128)}) %reduce-scatter.5.cloned.1.call-update) | async-done | bytes 184336
  176.3 29.3 %all_gather.11 = bf16[128,2880]{0,1:T(8,128)(2,1)S(1)} all-gather(bf16[128,360]{0,1:T(8,128)(2,1)S(1)} %add_convert_fusion), channel_id=1, replica_groups=mesh['req'=32,'tp'=8] {'tp'}, dimensions={1}, use_global_device_ids=true | all-gather | bytes 829440 | tf_op jit(solution)/shard_map/all_gather | solution.py:214
  206.0 4.0 convolution_convert_fusion
  210.0 6.5 %copy.131 = bf16[768,2880]{1,0:T(8,128)(2,1)} copy(bf16[768,2880]{0,1:T(8,128)(2,1)} %convolution_convert_fusion) | data formatting | bytes 8847360 | tf_op jit(solution)/shard_map/convert_element_type | solution.py:223
  216.6 9.4 %all-to-all-start = ((bf16[32,24,2880]{2,1,0:T(8,128)(2,1)}), bf16[32,24,2880]{2,1,0:T(8,128)(2,1)}, u32[]{:S(2)}, u32[]{:S(2)}) async-start(bf16[32,24,2880]{2,1,0:T(8,128)(2,1)} %bitcast.95), calls=%async_computation | async-start | bytes 9043968 | tf_op jit(solution)/shard_map/all_to_all | solution.py:224
  226.0 4.7 reshape.357
  230.7 98.9 %all-to-all-done = bf16[32,24,2880]{2,1,0:T(8,128)(2,1)} async-done(((bf16[32,24,2880]{2,1,0:T(8,128)(2,1)}), bf16[32,24,2880]{2,1,0:T(8,128)(2,1)}, u32[]{:S(2)}, u32[]{:S(2)}) %all-to-all-start) | async-done | bytes 4423712 | tf_op jit(solution)/shard_map/all_to_all | solution.py:224
  329.6 7.0 %convolution_bitcast_fusion.1 = f32[32,1,24,720]{3,2,0,1:T(8,128)S(1)} fusion(bf16[32,24,2880]{2,1,0:T(8,128)(2,1)} %all-to-all-done, bf16[2880,720,1]{0,1,2:T(8,128)(2,1)} %bitcast.111), kind=kOutput, calls=%fused_computation.10 | convolution fusion | flops 3185049600 | bytes 10782720 | tf_op jit(solution)/shard_map/sepd,edf->sepf/dot_general | solution.py:233
  336.6 4.8 %convolution_convert_fusion.1 = bf16[32,24,8,360]{3,1,2,0:T(8,128)(2,1)} fusion(bf16[360,8,360]{2,1,0:T(8,128)(2,1)S(1)} %reshape.357, f32[32,1,24,720]{3,2,0,1:T(8,128)S(1)} %convolution_bitcast_fusion.1), kind=kOutput, calls=%fused_computation.3 | convolution fusion | flops 1597501440 | bytes 8709120 | tf_op jit(solution)/shard_map/sepf,eftd->setpd/dot_general | solution.py:243
  341.4 11.9 %all-to-all-start.1 = ((bf16[256,24,360]{2,1,0:T(8,128)(2,1)}), bf16[256,24,360]{2,1,0:T(8,128)(2,1)}, u32[]{:S(2)}, u32[]{:S(2)}) async-start(bf16[256,24,360]{2,1,0:T(8,128)(2,1)} %bitcast.97), calls=%async_computation.1 | async-start | bytes 9437184 | tf_op jit(solution)/shard_map/all_to_all | solution.py:249
  354.8 1.5 fusion.26
  356.3 3.7 gather_fusion
  361.3 99.9 %all-to-all-done.1 = bf16[256,24,360]{2,1,0:T(8,128)(2,1)} async-done(((bf16[256,24,360]{2,1,0:T(8,128)(2,1)}), bf16[256,24,360]{2,1,0:T(8,128)(2,1)}, u32[]{:S(2)}, u32[]{:S(2)}) %all-to-all-start.1) | async-done | bytes 4423712 | tf_op jit(solution)/shard_map/all_to_all | solution.py:249
  461.4 7.8 %fusion.14 = bf16[128,360]{0,1:T(8,128)(2,1)} fusion(f32[128,6144]{0,1:T(8,128)S(1)} %bitcast.96, bf16[6144,360]{1,0:T(8,128)(2,1)} %bitcast.40, pred[128]{0:T(512)(128)(4,1)S(1)} %iota_compare_fusion.4), kind=kOutput, calls=%fused_computation.29 | convolution fusion | flops 3397478400 | bytes 7661696 | tf_op jit(solution)/shard_map/dot_general | solution.py:261
  (81 shorter events, 15.6 us)
Async XLA Ops:
  7.2 43.2 %copy-start = (bf16[2880,512]{1,0:T(8,128)(2,1)S(1)}, bf16[2880,512]{1,0:T(8,128)(2,1)}, u32[]{:S(2)}) copy-start(bf16[2880,512]{1,0:T(8,128)(2,1)} %param.16) | copy-start | bytes 8847364
  7.2 85.5 %all-gather.3.cloned.1.call-start = ((), (), s32[]{:S(2)}) async-start(), calls=%async_computation.3 | async-start | bytes 8650752 | tf_op jit(solution)/shard_map/all_gather | solution.py:182
  7.9 167.5 %reduce-scatter.5.cloned.1.call-start = ((), (), s32[]{:S(2)}) async-start(), calls=%async_computation.4 | async-start | bytes 1658880
  46.1 4.2 copy-start.8
  53.1 2.8 copy-start.7
  56.8 7.2 %copy-start.2 = (f32[1024,1]{1,0:T(8,128)}, f32[1024,1]{1,0:T(8,128)S(1)}, u32[]{:S(2)}) copy-start(f32[1024,1]{1,0:T(8,128)S(1)} %copy.121.m0_ref) | copy-start | bytes 12292
  57.7 4.6 copy-start.9
  127.7 5.4 %copy-start.5 = (s32[128,4]{0,1:T(4,128)S(1)}, s32[128,4]{0,1:T(4,128)}, u32[]{:S(2)}) copy-start(s32[128,4]{0,1:T(4,128)} %param.25) | copy-start | bytes 6148
  133.1 42.3 %copy-start.4 = (bf16[128,360]{0,1:T(8,128)(2,1)S(1)}, bf16[128,360]{0,1:T(8,128)(2,1)}, u32[]{:S(2)}) copy-start(bf16[128,360]{0,1:T(8,128)(2,1)} %param.14) | copy-start | bytes 276484
  133.1 72.9 %copy-start.6 = (f32[2880]{0:T(1024)S(1)}, f32[2880]{0:T(1024)}, u32[]{:S(2)}) copy-start(f32[2880]{0:T(1024)} %param.21) | copy-start | bytes 34564
  216.6 113.0 %all-to-all-start = ((bf16[32,24,2880]{2,1,0:T(8,128)(2,1)}), bf16[32,24,2880]{2,1,0:T(8,128)(2,1)}, u32[]{:S(2)}, u32[]{:S(2)}) async-start(bf16[32,24,2880]{2,1,0:T(8,128)(2,1)} %bitcast.95), calls=%async_computation | async-start | bytes 9043968 | tf_op jit(solution)/shard_map/all_to_all | solution.py:224
  341.4 12.1 %copy-start.10 = (s32[32]{0:T(128)S(1)}, s32[32]{0:T(128)}, u32[]{:S(2)}) copy-start(s32[32]{0:T(128)} %param.27) | copy-start | bytes 388
  341.4 119.8 %all-to-all-start.1 = ((bf16[256,24,360]{2,1,0:T(8,128)(2,1)}), bf16[256,24,360]{2,1,0:T(8,128)(2,1)}, u32[]{:S(2)}, u32[]{:S(2)}) async-start(bf16[256,24,360]{2,1,0:T(8,128)(2,1)} %bitcast.97), calls=%async_computation.1 | async-start | bytes 9437184 | tf_op jit(solution)/shard_map/all_to_all | solution.py:249
  356.3 4.4 copy-start.3
  461.4 7.8 %copy-start.1 = (bf16[2880,512]{1,0:T(8,128)(2,1)S(1)}, bf16[2880,512]{1,0:T(8,128)(2,1)}, u32[]{:S(2)}) copy-start(bf16[2880,512]{1,0:T(8,128)(2,1)} %param.16) | copy-start | bytes 8847364
Sparse Core Ops, SparseCore 0:
  10.6 82.1 all-gather.2
  133.2 42.1 reduce-scatter.4
